TPU v7x, 512 devices: a whole 4x8x8 slice. The times are simulated.
512 devices in a mesh: head: 8 (over y), blk: 64 (over z, x, core).
Axes of the slice: x: 4, y: 8, z: 8, core: 2. Of those that a mesh axis runs over, the one named last changes fastest.
Arguments:
- inputs: bfloat16 [4, 64, 7168], P(None, None, 'blk'), may hold values from -40 to 40
- ln_gain: bfloat16 [7168], P('blk'), may hold values from 0.099609375 to 1.8984375
- ln_bias: bfloat16 [7168], P('blk'), may hold values from -3 to 3
- w_query: bfloat16 [7168, 7168], P('blk', 'head'), may hold values from -0.0625 to 0.0625
- w_key: bfloat16 [7168, 7168], P('blk', 'head'), may hold values from -0.0625 to 0.0625
- w_value: bfloat16 [7168, 7168], P('blk', 'head'), may hold values from -0.0625 to 0.0625
- b_query: bfloat16 [7168], P('head'), may hold values from -3 to 3
- b_key: bfloat16 [7168], P('head'), may hold values from -4 to 4
- b_value: bfloat16 [7168], P('head'), may hold values from -3 to 3
- w_out: bfloat16 [7168, 7168], P('head', 'blk'), may hold values from -0.5 to 0.5
- b_out: bfloat16 [7168], P('blk'), may hold values from -3 to 3
- prefix_keys: bfloat16 [1536, 16, 7168], P('blk', None, 'head'), may hold values from -110 to 110
- prefix_values: bfloat16 [1536, 16, 7168], P('blk', None, 'head'), may hold values from -6 to 6
- suffix_keys: bfloat16 [64, 256, 7168], P('blk', None, 'head'), may hold values from -110 to 110
- suffix_values: bfloat16 [64, 256, 7168], P('blk', None, 'head'), may hold values from -6 to 6
- page_table: int32 [8, 288], replicated, may hold values from 0 to 1535, as said below
- prompt_len: int32 [8], replicated, may hold values from 1 to 4608, as said below
- gen_len: int32 [8], replicated, may hold values from 1 to 252, as said below
- parents: int32 [4, 64], replicated, may hold values from 0 to 63, as said below
Outputs:
- hidden: bfloat16 [4, 64, 7168], P(None, None, 'blk')
- final_keys: bfloat16 [64, 256, 7168], P('blk', None, 'head')
- final_values: bfloat16 [64, 256, 7168], P('blk', None, 'head')
Inputs may be any that keep to these rules, and one draw needn't show every extreme that they name: `page_table`: the first ceil(prompt_len[r] / 16) entries of row r are distinct pages that no other request lists; later entries are 0 and hold no tokens of r. `prompt_len`: the longest request has exactly 4608 tokens. `gen_len`: some request has exactly 252. parents[s, b] is a beam of the same request as b.
All inputs are finite; a program needn't handle non-finite values.
Results may differ from a plain program's by a relative error of at most 0.0065.
The roundings to bfloat16 on the way count: a program that leaves them out, or rounds other values in their place, can miss the bound.
Values may be sent and summed in bfloat16 or wider, within the bound.
No kernel may reach another device: no remote copies, remote signals or barrier semaphores. Data moves between devices by JAX's collectives and lax.ppermute only.
A program may use at most 128 MiB of HBM per device.

v0:
```python
import math

import jax
import jax.numpy as jnp
from jax import lax
from jax.sharding import PartitionSpec as P

D = 7168
HEAD_DIM = 128
BEAMS = 8
PAGE = 16
GEN = 256
STEPS = 4


MASKED = -1e30
NORM_EPSILON = 1e-05


def spread_rows(local, start, total_rows, fill_value):
    base = jnp.full((total_rows,) + local.shape[1:], fill_value, local.dtype)
    return lax.dynamic_update_slice_in_dim(base, local, start, 0)


def body(
    inputs,
    ln_gain,
    ln_bias,
    w_query,
    w_key,
    w_value,
    b_query,
    b_key,
    b_value,
    w_out,
    b_out,
    prefix_keys,
    prefix_values,
    suffix_keys,
    suffix_values,
    page_table,
    prompt_len,
    gen_len,
    parents,
):
    blocks = lax.axis_size("blk")
    blk_index = lax.axis_index("blk")
    local_beams = suffix_keys.shape[0]
    batch = local_beams * blocks
    feat_here = w_query.shape[1]
    heads_here = feat_here // HEAD_DIM
    pages_here = prefix_keys.shape[0]
    requests = page_table.shape[0]
    slot_count = page_table.shape[1]
    score_scale = 1.0 / math.sqrt(HEAD_DIM)
    first_beam = blk_index * local_beams
    beam_request = jnp.arange(batch, dtype=jnp.int32) // BEAMS
    local_request = lax.dynamic_slice_in_dim(beam_request, first_beam, local_beams)
    beam_prompt = jnp.take(prompt_len, beam_request)
    local_generated = jnp.take(gen_len, local_request)
    gen_rows = jnp.arange(GEN, dtype=jnp.int32)
    page_ids = blk_index * pages_here + jnp.arange(pages_here, dtype=jnp.int32)
    slot_ids = jnp.arange(slot_count, dtype=jnp.int32)
    slot_live = slot_ids[None, :] * PAGE < prompt_len[:, None]
    page_match = (
        (page_table[:, :, None] == page_ids[None, None, :]) & slot_live[:, :, None]
    ).astype(jnp.int32)
    request_ids = jnp.arange(requests, dtype=jnp.int32)
    page_request = jnp.sum(page_match * request_ids[:, None, None], axis=(0, 1))
    page_slot = jnp.sum(page_match * slot_ids[None, :, None], axis=(0, 1))
    page_used = jnp.sum(page_match, axis=(0, 1)) > 0
    token_pos = (page_slot[:, None] * PAGE + jnp.arange(PAGE, dtype=jnp.int32)[None, :]).reshape(-1)
    token_request = jnp.repeat(page_request, PAGE)
    token_used = jnp.repeat(page_used, PAGE)
    prefix_live = (
        token_used[None, :]
        & (token_request[None, :] == beam_request[:, None])
        & (token_pos[None, :] < beam_prompt[:, None])
    )
    page_keys = prefix_keys.reshape(pages_here * PAGE, heads_here, HEAD_DIM)
    page_values = prefix_values.reshape(pages_here * PAGE, heads_here, HEAD_DIM)
    weights_all = jnp.concatenate([w_query, w_key, w_value], axis=1)
    bias_all = jnp.concatenate([b_query, b_key, b_value]).astype(jnp.float32)
    norm_gain = ln_gain.astype(jnp.float32)
    norm_shift = ln_bias.astype(jnp.float32)
    beam_keys = suffix_keys
    beam_values = suffix_values
    hidden_steps = []
    for step_index in range(STEPS):
        rows_in = inputs[step_index].astype(jnp.float32)
        row_sum, row_squares = lax.psum(
            (jnp.sum(rows_in, axis=1), jnp.sum(rows_in * rows_in, axis=1)), "blk"
        )
        row_mean = row_sum / D
        variance = row_squares / D - row_mean * row_mean
        normed = (
            (rows_in - row_mean[:, None]) * lax.rsqrt(variance + NORM_EPSILON)[:, None] * norm_gain
            + norm_shift
        ).astype(jnp.bfloat16)
        partial_value = jnp.dot(normed, weights_all, preferred_element_type=jnp.float32)
        projected = (lax.psum(partial_value, "blk") + bias_all[None, :]).astype(jnp.bfloat16)
        queries = projected[:, :feat_here].reshape(batch, heads_here, HEAD_DIM)
        key_new = projected[:, feat_here : 2 * feat_here]
        value_new = projected[:, 2 * feat_here :]
        prompt_scores = (
            jnp.einsum("bhd,thd->bht", queries, page_keys, preferred_element_type=jnp.float32)
            * score_scale
        )
        local_top = jnp.max(jnp.where(prefix_live[:, None, :], prompt_scores, MASKED), axis=2)
        exchanged = (
            lax.all_to_all(beam_keys, "blk", split_axis=1, concat_axis=0, tiled=True),
            lax.all_to_all(beam_values, "blk", split_axis=1, concat_axis=0, tiled=True),
        )
        parent_order = parents[step_index]
        picked = (
            jnp.take(exchanged[0], parent_order, axis=0),
            jnp.take(exchanged[1], parent_order, axis=0),
        )
        beam_keys, beam_values = (
            lax.all_to_all(picked[0], "blk", split_axis=0, concat_axis=1, tiled=True),
            lax.all_to_all(picked[1], "blk", split_axis=0, concat_axis=1, tiled=True),
        )
        write_pos = local_generated + step_index
        written = (gen_rows[None, :] == write_pos[:, None])[:, :, None]
        beam_keys = jnp.where(
            written,
            lax.dynamic_slice_in_dim(key_new, first_beam, local_beams)[:, None, :],
            beam_keys,
        )
        beam_values = jnp.where(
            written,
            lax.dynamic_slice_in_dim(value_new, first_beam, local_beams)[:, None, :],
            beam_values,
        )
        own_queries = lax.dynamic_slice_in_dim(queries, first_beam, local_beams)
        cache_scores = (
            jnp.einsum(
                "bhd,bthd->bht",
                own_queries,
                beam_keys.reshape(local_beams, GEN, heads_here, HEAD_DIM),
                preferred_element_type=jnp.float32,
            )
            * score_scale
        )
        cache_live = (gen_rows[None, :] <= write_pos[:, None])[:, None, :]
        cache_top = jnp.max(jnp.where(cache_live, cache_scores, MASKED), axis=2)
        local_top = jnp.maximum(local_top, spread_rows(cache_top, first_beam, batch, MASKED))
        global_top = lax.pmax(local_top, "blk")
        prompt_weights = jnp.where(
            prefix_live[:, None, :], jnp.exp(prompt_scores - global_top[:, :, None]), 0.0
        ).astype(jnp.bfloat16)
        weighted = jnp.einsum(
            "bht,thd->bhd", prompt_weights, page_values, preferred_element_type=jnp.float32
        )
        totals = jnp.sum(prompt_weights.astype(jnp.float32), axis=2)
        own_top = lax.dynamic_slice_in_dim(global_top, first_beam, local_beams)
        cache_weights = jnp.where(
            cache_live, jnp.exp(cache_scores - own_top[:, :, None]), 0.0
        ).astype(jnp.bfloat16)
        cache_weighted = jnp.einsum(
            "bht,bthd->bhd",
            cache_weights,
            beam_values.reshape(local_beams, GEN, heads_here, HEAD_DIM),
            preferred_element_type=jnp.float32,
        )
        weighted = weighted + spread_rows(cache_weighted, first_beam, batch, 0.0)
        totals = totals + spread_rows(
            jnp.sum(cache_weights.astype(jnp.float32), axis=2), first_beam, batch, 0.0
        )
        weighted, totals = lax.psum((weighted, totals), "blk")
        attention = (weighted / totals[:, :, None]).reshape(batch, feat_here).astype(jnp.bfloat16)
        head_terms = jnp.dot(attention, w_out, preferred_element_type=jnp.float32)
        head_total = lax.psum(head_terms, "head")
        hidden_steps.append((head_total + b_out.astype(jnp.float32)[None, :]).astype(jnp.bfloat16))
    return (jnp.stack(hidden_steps, axis=0), beam_keys, beam_values)


def solution(mesh):
    in_specs = (
        P(None, None, "blk"),
        P("blk"),
        P("blk"),
        P("blk", "head"),
        P("blk", "head"),
        P("blk", "head"),
        P("head"),
        P("head"),
        P("head"),
        P("head", "blk"),
        P("blk"),
        P("blk", None, "head"),
        P("blk", None, "head"),
        P("blk", None, "head"),
        P("blk", None, "head"),
        P(),
        P(),
        P(),
        P(),
    )
    out_specs = (P(None, None, "blk"), P("blk", None, "head"), P("blk", None, "head"))
    return jax.shard_map(body, mesh=mesh, in_specs=in_specs, out_specs=out_specs, check_vma=False)
```

profile of v0, /device:TPU:1, one launch (start us, length us, event | category | flops | bytes accessed | tf_op | source)
XLA Modules:
  0.0 1312.4 jit_solution(7064974290930923964)
XLA Ops:
  14.1 15.0 %all-to-all-start = ((bf16[64,2,1792]{2,1,0:T(2,128)(2,1)}), bf16[64,2,1792]{2,1,0:T(2,128)(2,1)S(1)}, u32[]{:S(2)}, u32[]{:S(2)}) async-start(bf16[64,2,1792]{2,1,0:T(2,128)(2,1)} %reshape.1271), calls=%async_computation | async-start | bytes 917504 | tf_op jit(solution)/shard_map/all_to_all | solution.py:111
  29.4 128.7 %all-reduce.1 = (f32[64]{0:T(128)S(1)}, f32[64]{0:T(128)S(1)}, f32[64]{0:T(128)S(1)}, f32[64]{0:T(128)S(1)}, f32[64]{0:T(128)S(1)}, /*index=5*/f32[64]{0:T(128)S(1)}, f32[64]{0:T(128)S(1)}, f32[64]{0:T(128)S(1)}) all-reduce(f32[64]{0:T(128)S(1)} %get-tuple-element.22, ...), channel_id=1, replica_groups=mesh['head'=8,'blk'=64] {'blk'}, use_global_device_ids=true, to_apply=%region_45.47 | all-reduce | flops 512 | bytes 4096 | tf_op jit(solution)/shard_map/psum | solution.py:91
  167.1 10.9 all-to-all-start.2
  184.9 9.4 all-to-all-done.2
  218.4 6.4 all-to-all-done.1
  224.9 6.3 all-to-all-start.3
  231.1 162.0 %all-reduce.12.cloned.1.call-done = (f32[64,2688]{1,0:T(8,128)}, f32[64,2688]{1,0:T(8,128)}, f32[64,2688]{1,0:T(8,128)}, f32[64,2688]{1,0:T(8,128)}) async-done(((f32[64,2688]{1,0:T(8,128)}, f32[64,2688]{1,0:T(8,128)}, f32[64,2688]{1,0:T(8,128)}, f32[64,2688]{1,0:T(8,128)}), (f32[64,2688]{1,0:T(8,128)}, f32[64,2688]{1,0:T(8,128)}, f32[64,2688]{1,0:T(8,128)}, ...) | async-done | bytes 2752528 | tf_op jit(solution)/shard_map/psum | solution.py:101
  403.1 9.4 all-to-all-start.6
  417.8 11.1 all-to-all-done.6
  438.0 13.1 all-to-all-done.4
  457.5 21.8 %all_to_all.216 = bf16[64,4,896]{2,1,0:T(4,128)(2,1)S(1)} all-to-all(bf16[64,4,896]{2,1,0:T(4,128)(2,1)S(1)} %get-tuple-element.127), channel_id=1, replica_groups=mesh['head'=8,'blk'=64] {'blk'}, dimensions={0} | all-to-all | bytes 917504 | tf_op jit(solution)/shard_map/all_to_all | solution.py:120
  486.3 15.3 %all-to-all-done.7 = bf16[64,4,896]{2,1,0:T(4,128)(2,1)S(1)} async-done(((bf16[64,4,896]{2,1,0:T(4,128)(2,1)}), bf16[64,4,896]{2,1,0:T(4,128)(2,1)S(1)}, u32[]{:S(2)}, u32[]{:S(2)}) %all-to-all-start.7) | async-done | bytes 458784 | tf_op jit(solution)/shard_map/all_to_all | solution.py:121
  520.0 9.8 all-to-all-done.10
  529.9 6.2 all-to-all-start.8
  540.2 12.1 all-to-all-done.8
  569.1 11.9 all-to-all-done.9
  581.0 6.1 all-to-all-start.11
  590.9 12.4 all-to-all-done.11
  631.9 7.9 all-to-all-start.12
  672.5 8.9 all-to-all-start.13
  691.7 6.1 all-to-all-done.13
  725.6 242.6 %all-reduce.4 = (f32[64,7]{0,1:T(8,128)S(1)}, f32[64,7]{0,1:T(8,128)S(1)}, f32[64,7]{0,1:T(8,128)S(1)}, f32[64,7]{0,1:T(8,128)S(1)}) all-reduce(f32[64,7]{0,1:T(8,128)S(1)} %max.23, f32[64,7]{0,1:T(8,128)S(1)} %max.22, f32[64,7]{0,1:T(8,128)S(1)} %max.21, f32[64,7]{0,1:T(8,128)S(1)} %max.20), channel_id=1, replica_groups=mesh['head'=8,'blk'=64] {'blk'}, use_global_device_ids=true, to_apply=%region_49.51 | all-reduce | flops 1792 | bytes 14336 | tf_op jit(solution)/shard_map/pmax | solution.py:148
  979.0 246.1 %all-reduce = (f32[64,7]{0,1:T(8,128)S(1)}, f32[64,7]{0,1:T(8,128)S(1)}, f32[64,7]{0,1:T(8,128)S(1)}, f32[64,7]{0,1:T(8,128)S(1)}) all-reduce(f32[64,7]{0,1:T(8,128)S(1)} %add.328, f32[64,7]{0,1:T(8,128)S(1)} %add.321, f32[64,7]{0,1:T(8,128)S(1)} %add.314, f32[64,7]{0,1:T(8,128)S(1)} %add.306), channel_id=1, replica_groups=mesh['head'=8,'blk'=64] {'blk'}, use_global_device_ids=true, to_apply=%region_53.55 | all-reduce | flops 1792 | bytes 14336 | tf_op jit(solution)/shard_map/psum | solution.py:170
  1230.8 72.5 %all-reduce.14.cloned.1.call-done = (f32[64,112]{1,0:T(8,128)}, f32[64,112]{1,0:T(8,128)}, f32[64,112]{1,0:T(8,128)}, f32[64,112]{1,0:T(8,128)}) async-done(((f32[64,112]{1,0:T(8,128)}, f32[64,112]{1,0:T(8,128)}, f32[64,112]{1,0:T(8,128)}, f32[64,112]{1,0:T(8,128)}), (f32[64,112]{1,0:T(8,128)}, f32[64,112]{1,0:T(8,128)}, f32[64,112]{1,0:T(8,128)}, f32[64,112]{1,0:T(8,128)})) %all-reduce.14.cloned.1.call-update) | async-done | bytes 114704 | tf_op jit(solution)/shard_map/psum | solution.py:173
  (411 shorter events, 242.4 us)
Async XLA Ops:
  7.2 1217.9 %copy-start = (bf16[896,112]{0,1:T(8,128)(2,1)S(1)}, bf16[896,112]{0,1:T(8,128)(2,1)}, u32[]{:S(2)}) copy-start(bf16[896,112]{0,1:T(8,128)(2,1)} %param.30) | copy-start | bytes 602116
  14.1 153.0 %all-to-all-start = ((bf16[64,2,1792]{2,1,0:T(2,128)(2,1)}), bf16[64,2,1792]{2,1,0:T(2,128)(2,1)S(1)}, u32[]{:S(2)}, u32[]{:S(2)}) async-start(bf16[64,2,1792]{2,1,0:T(2,128)(2,1)} %reshape.1271), calls=%async_computation | async-start | bytes 917504 | tf_op jit(solution)/shard_map/all_to_all | solution.py:111
  29.1 129.1 %copy-start.35 = (bf16[112,896]{1,0:T(8,128)(2,1)S(1)}, bf16[112,896]{1,0:T(8,128)(2,1)}, u32[]{:S(2)}) copy-start(bf16[112,896]{1,0:T(8,128)(2,1)} %param.25) | copy-start | bytes 602116
  29.2 130.3 %copy-start.29 = (bf16[1,256,896]{2,1,0:T(8,128)(2,1)S(1)}, bf16[1,256,896]{2,1,0:T(8,128)(2,1)}, u32[]{:S(2)}) copy-start(bf16[1,256,896]{2,1,0:T(8,128)(2,1)} %param.35) | copy-start | bytes 1376260
  167.1 27.3 %all-to-all-start.2 = ((bf16[64,2,1792]{2,1,0:T(2,128)(2,1)}), bf16[64,2,1792]{2,1,0:T(2,128)(2,1)S(1)}, u32[]{:S(2)}, u32[]{:S(2)}) async-start(bf16[64,2,1792]{2,1,0:T(2,128)(2,1)} %reshape.1279), calls=%async_computation.2 | async-start | bytes 917504 | tf_op jit(solution)/shard_map/all_to_all | solution.py:112
  177.9 215.2 %all-reduce.12.cloned.1.call-start = ((), (), s32[]{:S(2)}) async-start(), calls=%async_computation.17 | async-start | bytes 5505024 | tf_op jit(solution)/shard_map/psum | solution.py:101
  200.8 16.9 %copy-start.59 = (bf16[896]{0:T(1024)(128)(2,1)S(1)}, bf16[896]{0:T(1024)(128)(2,1)}, u32[]{:S(2)}) copy-start(bf16[896]{0:T(1024)(128)(2,1)} %param.27) | copy-start | bytes 5380
  200.8 24.0 %all-to-all-start.1 = ((bf16[64,4,896]{2,1,0:T(4,128)(2,1)}), bf16[64,4,896]{2,1,0:T(4,128)(2,1)S(1)}, u32[]{:S(2)}, u32[]{:S(2)}) async-start(bf16[64,4,896]{2,1,0:T(4,128)(2,1)} %get-tuple-element.131), calls=%async_computation.1 | async-start | bytes 917504 | tf_op jit(solution)/shard_map/all_to_all | solution.py:120
  218.4 178.6 %copy-start.65 = (pred[256]{0:T(512)(128)(4,1)}, pred[256]{0:T(512)(128)(4,1)S(1)}, u32[]{:S(2)}) copy-start(pred[256]{0:T(512)(128)(4,1)S(1)} %iota_compare_fusion.6) | copy-start | bytes 772
  224.9 172.0 %all-to-all-start.3 = ((bf16[64,4,896]{2,1,0:T(4,128)(2,1)}), bf16[64,4,896]{2,1,0:T(4,128)(2,1)S(1)}, u32[]{:S(2)}, u32[]{:S(2)}) async-start(bf16[64,4,896]{2,1,0:T(4,128)(2,1)} %get-tuple-element.130), calls=%async_computation.3 | async-start | bytes 917504 | tf_op jit(solution)/shard_map/all_to_all | solution.py:121
  403.1 25.8 %all-to-all-start.6 = ((bf16[64,2,1792]{2,1,0:T(2,128)(2,1)}), bf16[64,2,1792]{2,1,0:T(2,128)(2,1)S(1)}, u32[]{:S(2)}, u32[]{:S(2)}) async-start(bf16[64,2,1792]{2,1,0:T(2,128)(2,1)} %reshape.1281), calls=%async_computation.6 | async-start | bytes 917504 | tf_op jit(solution)/shard_map/all_to_all | solution.py:112
  428.9 22.2 %all-to-all-start.4 = ((bf16[64,2,1792]{2,1,0:T(2,128)(2,1)}), bf16[64,2,1792]{2,1,0:T(2,128)(2,1)S(1)}, u32[]{:S(2)}, u32[]{:S(2)}) async-start(bf16[64,2,1792]{2,1,0:T(2,128)(2,1)} %reshape.1273), calls=%async_computation.4 | async-start | bytes 917504 | tf_op jit(solution)/shard_map/all_to_all | solution.py:111
  479.3 22.2 %all-to-all-start.7 = ((bf16[64,4,896]{2,1,0:T(4,128)(2,1)}), bf16[64,4,896]{2,1,0:T(4,128)(2,1)S(1)}, u32[]{:S(2)}, u32[]{:S(2)}) async-start(bf16[64,4,896]{2,1,0:T(4,128)(2,1)} %get-tuple-element.126), calls=%async_computation.7 | async-start | bytes 917504 | tf_op jit(solution)/shard_map/all_to_all | solution.py:121
  507.8 22.1 %all-to-all-start.10 = ((bf16[64,2,1792]{2,1,0:T(2,128)(2,1)}), bf16[64,2,1792]{2,1,0:T(2,128)(2,1)S(1)}, u32[]{:S(2)}, u32[]{:S(2)}) async-start(bf16[64,2,1792]{2,1,0:T(2,128)(2,1)} %reshape.1283), calls=%async_computation.10 | async-start | bytes 917504 | tf_op jit(solution)/shard_map/all_to_all | solution.py:112
  529.9 22.4 %all-to-all-start.8 = ((bf16[64,2,1792]{2,1,0:T(2,128)(2,1)}), bf16[64,2,1792]{2,1,0:T(2,128)(2,1)S(1)}, u32[]{:S(2)}, u32[]{:S(2)}) async-start(bf16[64,2,1792]{2,1,0:T(2,128)(2,1)} %reshape.1275), calls=%async_computation.8 | async-start | bytes 917504 | tf_op jit(solution)/shard_map/all_to_all | solution.py:111
  558.8 22.2 %all-to-all-start.9 = ((bf16[64,4,896]{2,1,0:T(4,128)(2,1)}), bf16[64,4,896]{2,1,0:T(4,128)(2,1)S(1)}, u32[]{:S(2)}, u32[]{:S(2)}) async-start(bf16[64,4,896]{2,1,0:T(4,128)(2,1)} %get-tuple-element.123), calls=%async_computation.9 | async-start | bytes 917504 | tf_op jit(solution)/shard_map/all_to_all | solution.py:120
  569.1 34.4 %copy-start.69 = (pred[256]{0:T(512)(128)(4,1)}, pred[256]{0:T(512)(128)(4,1)S(1)}, u32[]{:S(2)}) copy-start(pred[256]{0:T(512)(128)(4,1)S(1)} %iota_compare_fusion.2) | copy-start | bytes 772
  581.0 22.3 %all-to-all-start.11 = ((bf16[64,4,896]{2,1,0:T(4,128)(2,1)}), bf16[64,4,896]{2,1,0:T(4,128)(2,1)S(1)}, u32[]{:S(2)}, u32[]{:S(2)}) async-start(bf16[64,4,896]{2,1,0:T(4,128)(2,1)} %get-tuple-element.122), calls=%async_computation.11 | async-start | bytes 917504 | tf_op jit(solution)/shard_map/all_to_all | solution.py:121
  609.6 22.3 %all-to-all-start.14 = ((bf16[64,2,1792]{2,1,0:T(2,128)(2,1)}), bf16[64,2,1792]{2,1,0:T(2,128)(2,1)}, u32[]{:S(2)}, u32[]{:S(2)}) async-start(bf16[64,2,1792]{2,1,0:T(2,128)(2,1)} %reshape.1285), calls=%async_computation.14 | async-start | bytes 917504 | tf_op jit(solution)/shard_map/all_to_all | solution.py:112
  631.9 24.1 %all-to-all-start.12 = ((bf16[64,2,1792]{2,1,0:T(2,128)(2,1)}), bf16[64,2,1792]{2,1,0:T(2,128)(2,1)}, u32[]{:S(2)}, u32[]{:S(2)}) async-start(bf16[64,2,1792]{2,1,0:T(2,128)(2,1)} %reshape.1277), calls=%async_computation.12 | async-start | bytes 917504 | tf_op jit(solution)/shard_map/all_to_all | solution.py:111
  672.5 25.3 %all-to-all-start.13 = ((bf16[64,4,896]{2,1,0:T(4,128)(2,1)}), bf16[64,4,896]{2,1,0:T(4,128)(2,1)}, u32[]{:S(2)}, u32[]{:S(2)}) async-start(bf16[64,4,896]{2,1,0:T(4,128)(2,1)} %get-tuple-element.119), calls=%async_computation.13 | async-start | bytes 917504 | tf_op jit(solution)/shard_map/all_to_all | solution.py:120
  697.8 22.2 %all-to-all-start.15 = ((bf16[64,4,896]{2,1,0:T(4,128)(2,1)}), bf16[64,4,896]{2,1,0:T(4,128)(2,1)S(1)}, u32[]{:S(2)}, u32[]{:S(2)}) async-start(bf16[64,4,896]{2,1,0:T(4,128)(2,1)} %get-tuple-element.118), calls=%async_computation.15 | async-start | bytes 917504 | tf_op jit(solution)/shard_map/all_to_all | solution.py:121
  703.6 521.5 %all-reduce.10.cloned.1.call-start = ((), (), s32[]{:S(2)}) async-start(), calls=%async_computation.16 | async-start | bytes 1835008 | tf_op jit(solution)/shard_map/psum | solution.py:170
  976.9 326.3 %all-reduce.14.cloned.1.call-start = ((), (), s32[]{:S(2)}) async-start(), calls=%async_computation.18 | async-start | bytes 262144 | tf_op jit(solution)/shard_map/psum | solution.py:173
  (74 other events, 209.5 us)
Sparse Core Ops, SparseCore 0:
  182.6 210.4 all-reduce.11
  977.0 196.9 all-reduce.9
  1229.8 73.3 all-reduce.13
where the time goes:
time: 1330 us; the launch traced here: 1310 us
  blocking collectives  639 us (48%)
  waiting for transfers between devices  352 us (26%)
  starting transfers between devices  112 us (8%)
  local copies, waits for them, and re-layouts  107 us (8%)
  other arithmetic  65.5 us (5%)
  matrix products  18.6 us (1%)
  between operations  17.9 us (1%)
    psum x1, blocking collectives, body(): weighted, totals = lax.psum((weighted, totals), 'blk')  246 us
    pmax x1, blocking collectives, body(): global_top = lax.pmax(local_top, 'blk')  243 us
    psum x1, waiting for transfers between devices, body(): lax.psum(partial_value, 'blk') + bias_all[None, :]  162 us
    psum x1, blocking collectives, body(): lax.psum((jnp.sum(rows_in, axis=1), jnp.sum(rows_in * rows_in, axis=1)),...  129 us
    psum x1, waiting for transfers between devices, body(): head_total = lax.psum(head_terms, 'head')  72.5 us
    unnamed x181, local copies, waits for them, and re-layouts  40.6 us
    all_to_all x4, starting transfers between devices, body(): lax.all_to_all(beam_keys, 'blk', split_axis=1, concat_axis=0, tiled=True)  35 us
    all_to_all x4, waiting for transfers between devices, body(): lax.all_to_all(beam_values, 'blk', split_axis=1, concat_axis=0, tiled=True)  33.3 us
  transfers between devices with their start and end apart: 18, of which 15 were waited for; matrix products, arithmetic and copies ran while one was open for 7% of the time, Pallas kernels for 0%

commit v1 on v0

v1 whole, which is shorter than its diff:
```python
import math

import jax
import jax.numpy as jnp
import numpy as np
from jax import lax
from jax.sharding import Mesh
from jax.sharding import PartitionSpec as P

D = 7168
HEAD_DIM = 128
BEAMS = 8
PAGE = 16
GEN = 256
STEPS = 4

MASKED = -1e30
NORM_EPSILON = 1e-05

BLK_PARTS = ("z", "x", "core")
GROUP = ("x", "core")


def nested(reduce, value):
    for axis in reversed(BLK_PARTS):
        value = reduce(value, axis)
    return value


def blk_index():
    index = lax.axis_index("z")
    for axis in BLK_PARTS[1:]:
        index = index * lax.axis_size(axis) + lax.axis_index(axis)
    return index


def body(
    inputs,
    ln_gain,
    ln_bias,
    w_query,
    w_key,
    w_value,
    b_query,
    b_key,
    b_value,
    w_out,
    b_out,
    prefix_keys,
    prefix_values,
    suffix_keys,
    suffix_values,
    page_table,
    prompt_len,
    gen_len,
    parents,
):
    blocks = 1
    for axis in BLK_PARTS:
        blocks *= lax.axis_size(axis)
    me = blk_index()
    steps = inputs.shape[0]
    batch = inputs.shape[1]
    feat_here = w_query.shape[1]
    heads_here = feat_here // HEAD_DIM
    pages_here = prefix_keys.shape[0]
    requests = page_table.shape[0]
    slot_count = page_table.shape[1]
    rows = steps * batch
    score_scale = 1.0 / math.sqrt(HEAD_DIM)
    my_request = me // BEAMS
    first_beam = my_request * BEAMS
    my_gen = gen_len[my_request]

    beam_ids = jnp.arange(batch, dtype=jnp.int32)
    anc = {}
    for s in range(steps):
        x = beam_ids
        anc[(s, s)] = x
        for t in range(s, -1, -1):
            x = jnp.take(parents[t], x)
            anc[(t - 1, s)] = x
    origin = jnp.stack([anc[(-1, s)] for s in range(steps)])

    rows_in = inputs.astype(jnp.float32).reshape(rows, -1)
    stats = jnp.stack([jnp.sum(rows_in, axis=1), jnp.sum(rows_in * rows_in, axis=1)], axis=1)
    stats = nested(lax.psum, stats)
    row_mean = stats[:, 0] / D
    variance = stats[:, 1] / D - row_mean * row_mean
    normed = (
        (rows_in - row_mean[:, None]) * lax.rsqrt(variance + NORM_EPSILON)[:, None]
        * ln_gain.astype(jnp.float32)
        + ln_bias.astype(jnp.float32)
    ).astype(jnp.bfloat16)
    weights_all = jnp.concatenate([w_query, w_key, w_value], axis=1)
    bias_all = jnp.concatenate([b_query, b_key, b_value]).astype(jnp.float32)
    partial = jnp.dot(normed, weights_all, preferred_element_type=jnp.float32)
    projected = (nested(lax.psum, partial) + bias_all[None, :]).astype(jnp.bfloat16)
    queries = projected[:, :feat_here].reshape(steps, batch, heads_here, HEAD_DIM)
    key_new = projected[:, feat_here : 2 * feat_here].reshape(steps, batch, feat_here)
    value_new = projected[:, 2 * feat_here :].reshape(steps, batch, feat_here)

    beam_request = beam_ids // BEAMS
    beam_prompt = jnp.take(prompt_len, beam_request)
    page_ids = me * pages_here + jnp.arange(pages_here, dtype=jnp.int32)
    slot_ids = jnp.arange(slot_count, dtype=jnp.int32)
    slot_live = slot_ids[None, :] * PAGE < prompt_len[:, None]
    page_match = (
        (page_table[:, :, None] == page_ids[None, None, :]) & slot_live[:, :, None]
    ).astype(jnp.int32)
    request_ids = jnp.arange(requests, dtype=jnp.int32)
    page_request = jnp.sum(page_match * request_ids[:, None, None], axis=(0, 1))
    page_slot = jnp.sum(page_match * slot_ids[None, :, None], axis=(0, 1))
    page_used = jnp.sum(page_match, axis=(0, 1)) > 0
    token_pos = (page_slot[:, None] * PAGE + jnp.arange(PAGE, dtype=jnp.int32)[None, :]).reshape(-1)
    token_request = jnp.repeat(page_request, PAGE)
    token_used = jnp.repeat(page_used, PAGE)
    prefix_live = (
        token_used[None, :]
        & (token_request[None, :] == beam_request[:, None])
        & (token_pos[None, :] < beam_prompt[:, None])
    )
    page_keys = prefix_keys.reshape(pages_here * PAGE, heads_here, HEAD_DIM)
    page_values = prefix_values.reshape(pages_here * PAGE, heads_here, HEAD_DIM)
    flat_queries = queries.reshape(rows, heads_here, HEAD_DIM)
    prompt_scores = (
        jnp.einsum("rhd,thd->rht", flat_queries, page_keys, preferred_element_type=jnp.float32)
        * score_scale
    ).reshape(steps, batch, heads_here, -1)
    prompt_live = prefix_live[None, :, None, :]
    prompt_top = jnp.max(jnp.where(prompt_live, prompt_scores, MASKED), axis=3)

    group_queries = lax.dynamic_slice_in_dim(queries, first_beam, BEAMS, axis=1)
    group_origin = lax.dynamic_slice_in_dim(origin, first_beam, BEAMS, axis=1)
    own_keys = suffix_keys[0].reshape(GEN, heads_here, HEAD_DIM)
    own_values = suffix_values[0].reshape(GEN, heads_here, HEAD_DIM)
    cache_scores = (
        jnp.einsum("sbhd,jhd->sbhj", group_queries, own_keys, preferred_element_type=jnp.float32)
        * score_scale
    )
    gen_rows = jnp.arange(GEN, dtype=jnp.int32)
    cache_live = (group_origin == me)[:, :, None, None] & (gen_rows < my_gen)[None, None, None, :]
    cache_top = jnp.max(jnp.where(cache_live, cache_scores, MASKED), axis=3)

    own_beam = me
    own_queries = lax.dynamic_index_in_dim(queries, own_beam, axis=1, keepdims=False)
    new_src = jnp.stack(
        [jnp.stack([anc[(t, s)][own_beam] if t <= s else own_beam for t in range(steps)]) for s in range(steps)]
    )
    step_ids = jnp.arange(steps, dtype=jnp.int32)
    new_keys_here = key_new[step_ids[None, :], new_src].reshape(steps, steps, heads_here, HEAD_DIM)
    new_values_here = value_new[step_ids[None, :], new_src].reshape(steps, steps, heads_here, HEAD_DIM)
    new_scores = (
        jnp.einsum("shd,sthd->sht", own_queries, new_keys_here, preferred_element_type=jnp.float32)
        * score_scale
    )
    new_live = (step_ids[None, :] <= step_ids[:, None])[:, None, :]
    new_top = jnp.max(jnp.where(new_live, new_scores, MASKED), axis=2)

    local_top = prompt_top
    group_top = jnp.maximum(
        lax.dynamic_slice_in_dim(local_top, first_beam, BEAMS, axis=1), cache_top
    )
    local_top = lax.dynamic_update_slice_in_dim(local_top, group_top, first_beam, axis=1)
    own_top = jnp.maximum(lax.dynamic_index_in_dim(local_top, own_beam, axis=1, keepdims=True), new_top[:, None])
    local_top = lax.dynamic_update_slice_in_dim(local_top, own_top, own_beam, axis=1)
    top = nested(lax.pmax, local_top)

    prompt_weights = jnp.where(
        prompt_live, jnp.exp(prompt_scores - top[:, :, :, None]), 0.0
    ).astype(jnp.bfloat16)
    weighted = jnp.einsum(
        "rht,thd->rhd",
        prompt_weights.reshape(rows, heads_here, -1),
        page_values,
        preferred_element_type=jnp.float32,
    ).reshape(steps, batch, heads_here, HEAD_DIM)
    totals = jnp.sum(prompt_weights.astype(jnp.float32), axis=3)

    group_top_all = lax.dynamic_slice_in_dim(top, first_beam, BEAMS, axis=1)
    cache_weights = jnp.where(
        cache_live, jnp.exp(cache_scores - group_top_all[:, :, :, None]), 0.0
    ).astype(jnp.bfloat16)
    cache_weighted = jnp.einsum(
        "sbhj,jhd->sbhd", cache_weights, own_values, preferred_element_type=jnp.float32
    )
    cache_totals = jnp.sum(cache_weights.astype(jnp.float32), axis=3)

    own_top_all = lax.dynamic_index_in_dim(top, own_beam, axis=1, keepdims=False)
    new_weights = jnp.where(
        new_live, jnp.exp(new_scores - own_top_all[:, :, None]), 0.0
    ).astype(jnp.bfloat16)
    new_weighted = jnp.einsum(
        "sht,sthd->shd", new_weights, new_values_here, preferred_element_type=jnp.float32
    )
    new_totals = jnp.sum(new_weights.astype(jnp.float32), axis=2)

    group_weighted = lax.dynamic_slice_in_dim(weighted, first_beam, BEAMS, axis=1) + cache_weighted
    weighted = lax.dynamic_update_slice_in_dim(weighted, group_weighted, first_beam, axis=1)
    group_totals = lax.dynamic_slice_in_dim(totals, first_beam, BEAMS, axis=1) + cache_totals
    totals = lax.dynamic_update_slice_in_dim(totals, group_totals, first_beam, axis=1)
    own_weighted = lax.dynamic_index_in_dim(weighted, own_beam, axis=1, keepdims=True) + new_weighted[:, None]
    weighted = lax.dynamic_update_slice_in_dim(weighted, own_weighted, own_beam, axis=1)
    own_totals = lax.dynamic_index_in_dim(totals, own_beam, axis=1, keepdims=True) + new_totals[:, None]
    totals = lax.dynamic_update_slice_in_dim(totals, own_totals, own_beam, axis=1)

    lanes = 128
    packed = jnp.concatenate(
        [
            weighted.reshape(rows, feat_here),
            jnp.pad(totals.reshape(rows, heads_here), ((0, 0), (0, lanes - heads_here))),
        ],
        axis=1,
    )
    packed = nested(lax.psum, packed)
    weighted = packed[:, :feat_here].reshape(rows, heads_here, HEAD_DIM)
    totals = packed[:, feat_here : feat_here + heads_here]
    attention = (weighted / totals[:, :, None]).reshape(rows, feat_here).astype(jnp.bfloat16)
    head_terms = jnp.dot(attention, w_out, preferred_element_type=jnp.float32)
    head_total = lax.psum(head_terms, "head")
    hidden = (head_total + b_out.astype(jnp.float32)[None, :]).astype(jnp.bfloat16)
    hidden = hidden.reshape(steps, batch, -1)

    final_origin = origin[steps - 1]
    pick = lax.dynamic_slice_in_dim(final_origin, first_beam, BEAMS) - first_beam
    my_final_src = [anc[(t, steps - 1)][own_beam] for t in range(steps)]
    write_rows = my_gen + step_ids

    def reorder(cache, fresh):
        chunks = cache[0].reshape(BEAMS, GEN // BEAMS, feat_here)
        spread = lax.all_to_all(chunks, GROUP, 0, 0, tiled=True)
        picked = jnp.take(spread, pick, axis=0)
        back = lax.all_to_all(picked, GROUP, 0, 0, tiled=True).reshape(GEN, feat_here)
        new_rows = jnp.stack([fresh[t, my_final_src[t]] for t in range(steps)])
        hit = gen_rows[:, None] == write_rows[None, :]
        chosen = jnp.argmax(hit, axis=1)
        out = jnp.where(jnp.any(hit, axis=1)[:, None], jnp.take(new_rows, chosen, axis=0), back)
        return out[None]

    final_keys = reorder(suffix_keys, key_new)
    final_values = reorder(suffix_values, value_new)
    return hidden, final_keys, final_values


def solution(mesh):
    heads = mesh.shape["head"]
    blocks = mesh.shape["blk"]
    cores = 2
    group_chips = BEAMS // cores
    devices = np.asarray(mesh.devices).reshape(heads, blocks // BEAMS, group_chips, cores)
    fine = Mesh(devices, ("head",) + BLK_PARTS)
    blk = BLK_PARTS
    in_specs = (
        P(None, None, blk),
        P(blk),
        P(blk),
        P(blk, "head"),
        P(blk, "head"),
        P(blk, "head"),
        P("head"),
        P("head"),
        P("head"),
        P("head", blk),
        P(blk),
        P(blk, None, "head"),
        P(blk, None, "head"),
        P(blk, None, "head"),
        P(blk, None, "head"),
        P(),
        P(),
        P(),
        P(),
    )
    out_specs = (P(None, None, blk), P(blk, None, "head"), P(blk, None, "head"))
    return jax.shard_map(body, mesh=fine, in_specs=in_specs, out_specs=out_specs, check_vma=False)
```

time: 1330 us -> 612 us (0.46)
  blocking collectives: 639 us -> 73.4 us
  starting transfers between devices: 112 us -> 18.2 us
  local copies, waits for them, and re-layouts: 107 us -> 41.3 us
  waiting for transfers between devices: 352 us -> 415 us
  other arithmetic: 65.5 us -> 24.4 us
    psum x2 -> x3, blocking collectives: 375 us -> 31.5 us  [nested(): value = reduce(value, axis)]
    pmax x1 -> x3, blocking collectives: 243 us -> 41.9 us  [nested(): value = reduce(value, axis)]
    psum x2 -> x6, waiting for transfers between devices: 162 us -> 333 us  [nested(): value = reduce(value, axis)]
    all_to_all x15 -> x4, waiting for transfers between devices: 117 us -> 9.08 us  [the longest x2 7.18 us: reorder(): lax.all_to_all(picked, GROUP, 0, 0, tiled=True).reshape(GEN, feat_here)]
    all_to_all x15 -> x4, starting transfers between devices: 111 us -> 18 us  [the longest x2 10.2 us: reorder(): lax.all_to_all(picked, GROUP, 0, 0, tiled=True).reshape(GEN, feat_here)]
    all_to_all x32 -> x0, local copies, waits for them, and re-layouts: 37.2 us -> none  [the longest x8 14 us: body(): lax.all_to_all(beam_keys, 'blk', split_axis=1, concat_axis=0, tiled=True)]
    unnamed x181 -> x25, local copies, waits for them, and re-layouts: 40.6 us -> 4.22 us
    unnamed x8 -> x0, other arithmetic: 28.9 us -> none
  transfers between devices with their start and end apart: 18 -> 11, of which waited for: 15 -> 9; matrix products, arithmetic and copies ran while one was open for 7% -> 7% of each run, Pallas kernels for 0% -> 0%
where the time goes in v1:
time: 612 us; the launch traced here: 607 us
  waiting for transfers between devices  415 us (68%)
  blocking collectives  73.4 us (12%)
  local copies, waits for them, and re-layouts  41.3 us (7%)
  other arithmetic  24.4 us (4%)
  between operations  20.1 us (3%)
  starting transfers between devices  18.2 us (3%)
  matrix products  14.2 us (2%)
    psum x6, waiting for transfers between devices, nested(): value = reduce(value, axis)  333 us
    psum x1, waiting for transfers between devices, body(): head_total = lax.psum(head_terms, 'head')  72.9 us
    pmax x3, blocking collectives, nested(): value = reduce(value, axis)  41.9 us
    psum x3, blocking collectives, nested(): value = reduce(value, axis)  31.5 us
  transfers between devices with their start and end apart: 11, of which 9 were waited for; matrix products, arithmetic and copies ran while one was open for 7% of the time, Pallas kernels for 0%

profile of v1, /device:TPU:1, one launch (start us, length us, event | category | flops | bytes accessed | tf_op | source)
XLA Modules:
  0.0 606.6 jit_solution(4780817149313871015)
XLA Ops:
  9.7 9.0 %psum.70 = f32[256,2]{0,1:T(2,128)S(1)} all-reduce(f32[256,2]{0,1:T(2,128)S(1)} %pad_maximum_fusion.2), channel_id=1, replica_groups=mesh['head'=8,'z'=8,'x'=4,'core'=2] {'core'}, use_global_device_ids=true, to_apply=%region_5.6 | all-reduce | flops 512 | bytes 4096 | tf_op jit(solution)/shard_map/psum | solution.py:26
  18.7 6.1 psum.71
  24.8 16.4 %psum.72 = f32[256,2]{0,1:T(2,128)S(1)} all-reduce(f32[256,2]{0,1:T(2,128)S(1)} %psum.71), channel_id=1, replica_groups=mesh['head'=8,'z'=8,'x'=4,'core'=2] {'z'}, use_global_device_ids=true, to_apply=%region_7.8 | all-reduce | flops 512 | bytes 4096 | tf_op jit(solution)/shard_map/psum | solution.py:26
  42.2 3.2 fusion.12
  45.5 40.7 %all-reduce.9.cloned.1.call-done = f32[256,2688]{1,0:T(8,128)} async-done(((f32[256,2688]{1,0:T(8,128)}), f32[256,2688]{1,0:T(8,128)}) %all-reduce.9.cloned.1.call-update) | async-done | bytes 2752528 | tf_op jit(solution)/shard_map/psum | solution.py:26
  94.5 74.2 %all-reduce.11.cloned.1.call-done = f32[256,2688]{1,0:T(8,128)} async-done(((f32[256,2688]{1,0:T(8,128)}), f32[256,2688]{1,0:T(8,128)}) %all-reduce.11.cloned.1.call-update) | async-done | bytes 2752528 | tf_op jit(solution)/shard_map/psum | solution.py:26
  186.5 5.1 and_select_fusion.7
  191.8 70.4 %all-reduce.13.cloned.1.call-done = f32[256,2688]{1,0:T(8,128)} async-done(((f32[256,2688]{1,0:T(8,128)}), f32[256,2688]{1,0:T(8,128)}) %all-reduce.13.cloned.1.call-update) | async-done | bytes 2752528 | tf_op jit(solution)/shard_map/psum | solution.py:26
  266.7 2.1 fusion
  273.3 5.5 pmax.21
  278.9 13.5 %pmax.22 = f32[4,64,7]{1,0,2:T(4,128)S(1)} all-reduce(f32[4,64,7]{1,0,2:T(4,128)S(1)} %pmax.21), channel_id=1, replica_groups=mesh['head'=8,'z'=8,'x'=4,'core'=2] {'x'}, use_global_device_ids=true, to_apply=%region_15.17 | all-reduce | flops 1792 | bytes 14336 | tf_op jit(solution)/shard_map/pmax | solution.py:26
  292.4 22.8 %pmax.23 = f32[4,64,7]{1,0,2:T(4,128)S(1)} all-reduce(f32[4,64,7]{1,0,2:T(4,128)S(1)} %pmax.22), channel_id=1, replica_groups=mesh['head'=8,'z'=8,'x'=4,'core'=2] {'z'}, use_global_device_ids=true, to_apply=%region_16.18 | all-reduce | flops 1792 | bytes 14336 | tf_op jit(solution)/shard_map/pmax | solution.py:26
  318.4 2.9 fusion.8
  323.4 2.0 fusion.6
  331.0 45.2 %all-reduce.15.cloned.1.call-done = f32[256,1024]{1,0:T(8,128)} async-done(((f32[256,1024]{1,0:T(8,128)}), f32[256,1024]{1,0:T(8,128)}) %all-reduce.15.cloned.1.call-update) | async-done | bytes 1048592 | tf_op jit(solution)/shard_map/psum | solution.py:26
  376.3 3.6 all-to-all-start.2
  388.7 4.2 all-to-all-start
  393.0 43.3 %all-reduce.17.cloned.1.call-done = f32[256,1024]{1,0:T(8,128)} async-done(((f32[256,1024]{1,0:T(8,128)}), f32[256,1024]{1,0:T(8,128)}) %all-reduce.17.cloned.1.call-update) | async-done | bytes 1048592 | tf_op jit(solution)/shard_map/psum | solution.py:26
  438.6 5.9 all-to-all-start.3
  446.1 7.2 %all-to-all-done.3 = bf16[8,32,896]{2,1,0:T(8,128)(2,1)S(1)} async-done(((bf16[8,32,896]{2,1,0:T(8,128)(2,1)}), bf16[8,32,896]{2,1,0:T(8,128)(2,1)S(1)}, u32[]{:S(2)}, u32[]{:S(2)}) %all-to-all-start.3) | async-done | bytes 458784 | tf_op jit(solution)/shard_map/all_to_all | solution.py:233
  453.3 4.2 all-to-all-start.1
  460.0 59.1 %all-reduce.19.cloned.1.call-done = f32[256,1024]{1,0:T(8,128)} async-done(((f32[256,1024]{1,0:T(8,128)}), f32[256,1024]{1,0:T(8,128)}) %all-reduce.19.cloned.1.call-update) | async-done | bytes 1048592 | tf_op jit(solution)/shard_map/psum | solution.py:26
  521.5 2.4 fusion.18
  525.1 72.9 %all-reduce.21.cloned.1.call-done = f32[256,112]{0,1:T(8,128)} async-done(((f32[256,112]{0,1:T(8,128)}), f32[256,112]{0,1:T(8,128)}) %all-reduce.21.cloned.1.call-update) | async-done | bytes 114704 | tf_op jit(solution)/shard_map/psum | solution.py:220
  (178 shorter events, 64.5 us)
Async XLA Ops:
  7.2 514.3 %copy-start = (bf16[896,112]{0,1:T(8,128)(2,1)S(1)}, bf16[896,112]{0,1:T(8,128)(2,1)}, u32[]{:S(2)}) copy-start(bf16[896,112]{0,1:T(8,128)(2,1)} %param.34) | copy-start | bytes 602116
  7.2 79.0 %all-reduce.9.cloned.1.call-start = ((), (), s32[]{:S(2)}) async-start(), calls=%async_computation.4 | async-start | bytes 5505024 | tf_op jit(solution)/shard_map/psum | solution.py:26
  45.4 40.9 %copy-start.3 = (s32[8]{0:T(128)S(1)}, s32[8]{0:T(128)}, u32[]{:S(2)}) copy-start(s32[8]{0:T(128)} %param.41) | copy-start | bytes 100
  45.4 41.0 %copy-start.4 = (s32[8,288]{1,0:T(8,128)S(1)}, s32[8,288]{1,0:T(8,128)}, u32[]{:S(2)}) copy-start(s32[8,288]{1,0:T(8,128)} %param.40) | copy-start | bytes 27652
  45.4 41.8 %copy-start.1 = (bf16[24,16,896]{2,1,0:T(8,128)(2,1)S(1)}, bf16[24,16,896]{2,1,0:T(8,128)(2,1)}, u32[]{:S(2)}) copy-start(bf16[24,16,896]{2,1,0:T(8,128)(2,1)} %param.36) | copy-start | bytes 2064388
  45.4 43.5 %copy-start.8 = (s32[4,64]{1,0:T(4,128)S(1)}, s32[4,64]{1,0:T(4,128)}, u32[]{:S(2)}) copy-start(s32[4,64]{1,0:T(4,128)} %param.43) | copy-start | bytes 3076
  45.4 123.2 %all-reduce.11.cloned.1.call-start = ((), (), s32[]{:S(2)}) async-start(), calls=%async_computation.5 | async-start | bytes 5505024 | tf_op jit(solution)/shard_map/psum | solution.py:26
  86.2 175.9 %all-reduce.13.cloned.1.call-start = ((), (), s32[]{:S(2)}) async-start(), calls=%async_computation.6 | async-start | bytes 5505024 | tf_op jit(solution)/shard_map/psum | solution.py:26
  94.5 86.2 %copy-start.2 = (bf16[24,16,896]{2,1,0:T(8,128)(2,1)S(1)}, bf16[24,16,896]{2,1,0:T(8,128)(2,1)}, u32[]{:S(2)}) copy-start(bf16[24,16,896]{2,1,0:T(8,128)(2,1)} %param.37) | copy-start | bytes 2064388
  168.7 15.6 %copy-start.9 = (s32[8]{0:T(128)S(1)}, s32[8]{0:T(128)}, u32[]{:S(2)}) copy-start(s32[8]{0:T(128)} %param.42) | copy-start | bytes 100
  168.7 22.8 %copy-start.5 = (bf16[896]{0:T(1024)(128)(2,1)S(1)}, bf16[896]{0:T(1024)(128)(2,1)}, u32[]{:S(2)}) copy-start(bf16[896]{0:T(1024)(128)(2,1)} %param.33) | copy-start | bytes 5380
  168.7 22.8 %copy-start.6 = (bf16[896]{0:T(1024)(128)(2,1)S(1)}, bf16[896]{0:T(1024)(128)(2,1)}, u32[]{:S(2)}) copy-start(bf16[896]{0:T(1024)(128)(2,1)} %param.32) | copy-start | bytes 5380
  168.7 22.8 %copy-start.7 = (bf16[896]{0:T(1024)(128)(2,1)S(1)}, bf16[896]{0:T(1024)(128)(2,1)}, u32[]{:S(2)}) copy-start(bf16[896]{0:T(1024)(128)(2,1)} %param.31) | copy-start | bytes 5380
  168.7 207.5 %all-reduce.15.cloned.1.call-start = ((), (), s32[]{:S(2)}) async-start(), calls=%async_computation.7 | async-start | bytes 2097152 | tf_op jit(solution)/shard_map/psum | solution.py:26
  329.8 53.7 %copy-start.10 = (bf16[112]{0:T(256)(128)(2,1)S(1)}, bf16[112]{0:T(256)(128)(2,1)}, u32[]{:S(2)}) copy-start(bf16[112]{0:T(256)(128)(2,1)} %param.35) | copy-start | bytes 676
  331.0 105.3 %all-reduce.17.cloned.1.call-start = ((), (), s32[]{:S(2)}) async-start(), calls=%async_computation.8 | async-start | bytes 2097152 | tf_op jit(solution)/shard_map/psum | solution.py:26
  376.3 12.4 %all-to-all-start.2 = ((bf16[8,32,896]{2,1,0:T(8,128)(2,1)}), bf16[8,32,896]{2,1,0:T(8,128)(2,1)S(1)}, u32[]{:S(2)}, u32[]{:S(2)}) async-start(bf16[8,32,896]{2,1,0:T(8,128)(2,1)} %bitcast.68), calls=%async_computation.2 | async-start | bytes 917504 | tf_op jit(solution)/shard_map/all_to_all | solution.py:231
  388.7 48.2 %all-to-all-start = ((bf16[8,32,896]{2,1,0:T(8,128)(2,1)}), bf16[8,32,896]{2,1,0:T(8,128)(2,1)S(1)}, u32[]{:S(2)}, u32[]{:S(2)}) async-start(bf16[8,32,896]{2,1,0:T(8,128)(2,1)} %bitcast.61), calls=%async_computation | async-start | bytes 917504 | tf_op jit(solution)/shard_map/all_to_all | solution.py:231
  392.9 126.2 %all-reduce.19.cloned.1.call-start = ((), (), s32[]{:S(2)}) async-start(), calls=%async_computation.9 | async-start | bytes 2097152 | tf_op jit(solution)/shard_map/psum | solution.py:26
  438.6 14.7 %all-to-all-start.3 = ((bf16[8,32,896]{2,1,0:T(8,128)(2,1)}), bf16[8,32,896]{2,1,0:T(8,128)(2,1)S(1)}, u32[]{:S(2)}, u32[]{:S(2)}) async-start(bf16[8,32,896]{2,1,0:T(8,128)(2,1)} %get-tuple-element.45), calls=%async_computation.3 | async-start | bytes 917504 | tf_op jit(solution)/shard_map/all_to_all | solution.py:233
  453.3 70.6 %all-to-all-start.1 = ((bf16[8,32,896]{2,1,0:T(8,128)(2,1)}), bf16[8,32,896]{2,1,0:T(8,128)(2,1)S(1)}, u32[]{:S(2)}, u32[]{:S(2)}) async-start(bf16[8,32,896]{2,1,0:T(8,128)(2,1)} %get-tuple-element.46), calls=%async_computation.1 | async-start | bytes 917504 | tf_op jit(solution)/shard_map/all_to_all | solution.py:233
  457.6 140.5 %all-reduce.21.cloned.1.call-start = ((), (), s32[]{:S(2)}) async-start(), calls=%async_computation.10 | async-start | bytes 229376 | tf_op jit(solution)/shard_map/psum | solution.py:220
Sparse Core Ops, SparseCore 0:
  45.6 40.6 all-reduce.8
  88.7 79.9 all-reduce.10
  171.2 90.9 all-reduce.12
  331.1 45.1 all-reduce.14
  378.6 57.5 all-reduce.16
  438.4 80.6 all-reduce.18
  524.0 73.9 all-reduce.20

commit v2 on v1

--- a/solution.py
+++ b/solution.py
@@ -24,6 +24,45 @@
 def nested(reduce, value):
     for axis in reversed(BLK_PARTS):
         value = reduce(value, axis)
+    return value
+
+
+def halving_stages(axes):
+    stages = []
+    for axis in axes:
+        size = lax.axis_size(axis)
+        bit = 1
+        while bit < size:
+            stages.append((axis, bit))
+            bit *= 2
+    return stages
+
+
+def exchange(value, axis, bit):
+    size = lax.axis_size(axis)
+    return lax.ppermute(value, axis, [(i, i ^ bit) for i in range(size)])
+
+
+def upper_half(axis, bit):
+    return (lax.axis_index(axis) // bit) % 2 == 1
+
+
+def scatter_sum(value, stages, combine=jnp.add):
+    for axis, bit in stages:
+        half = value.shape[0] // 2
+        low, high = value[:half], value[half:]
+        upper = upper_half(axis, bit)
+        keep = jnp.where(upper, high, low)
+        send = jnp.where(upper, low, high)
+        value = combine(keep, exchange(send, axis, bit))
+    return value
+
+
+def gather_rows(value, stages):
+    for axis, bit in reversed(stages):
+        other = exchange(value, axis, bit)
+        upper = upper_half(axis, bit)
+        value = jnp.where(upper, jnp.concatenate([other, value]), jnp.concatenate([value, other]))
     return value
 
 
@@ -95,7 +134,9 @@
     weights_all = jnp.concatenate([w_query, w_key, w_value], axis=1)
     bias_all = jnp.concatenate([b_query, b_key, b_value]).astype(jnp.float32)
     partial = jnp.dot(normed, weights_all, preferred_element_type=jnp.float32)
-    projected = (nested(lax.psum, partial) + bias_all[None, :]).astype(jnp.bfloat16)
+    blk_stages = halving_stages(("core",) + GROUP[:1] + ("z",))
+    projected = (scatter_sum(partial, blk_stages) + bias_all[None, :]).astype(jnp.bfloat16)
+    projected = gather_rows(projected, blk_stages)
     queries = projected[:, :feat_here].reshape(steps, batch, heads_here, HEAD_DIM)
     key_new = projected[:, feat_here : 2 * feat_here].reshape(steps, batch, feat_here)
     value_new = projected[:, 2 * feat_here :].reshape(steps, batch, feat_here)
@@ -212,12 +253,15 @@
         ],
         axis=1,
     )
-    packed = nested(lax.psum, packed)
-    weighted = packed[:, :feat_here].reshape(rows, heads_here, HEAD_DIM)
+    packed = scatter_sum(packed, blk_stages)
+    part_rows = packed.shape[0]
+    weighted = packed[:, :feat_here].reshape(part_rows, heads_here, HEAD_DIM)
     totals = packed[:, feat_here : feat_here + heads_here]
-    attention = (weighted / totals[:, :, None]).reshape(rows, feat_here).astype(jnp.bfloat16)
+    attention = (weighted / totals[:, :, None]).reshape(part_rows, feat_here).astype(jnp.bfloat16)
+    attention = gather_rows(attention, blk_stages)
     head_terms = jnp.dot(attention, w_out, preferred_element_type=jnp.float32)
-    head_total = lax.psum(head_terms, "head")
+    head_stages = halving_stages(("head",))
+    head_total = gather_rows(scatter_sum(head_terms, head_stages), head_stages)
     hidden = (head_total + b_out.astype(jnp.float32)[None, :]).astype(jnp.bfloat16)
     hidden = hidden.reshape(steps, batch, -1)
 

time: 612 us -> 391 us (0.64)
  waiting for transfers between devices: 415 us -> 94.6 us
  starting transfers between devices: 18.2 us -> 143 us
  between operations: 20.1 us -> 7.55 us
    psum x7 -> x0, waiting for transfers between devices: 406 us -> none  [the longest x6 333 us: nested(): value = reduce(value, axis)]
    ppermute x0 -> x30, starting transfers between devices: none -> 112 us  [exchange(): return lax.ppermute(value, axis, [(i, i ^ bit) for i in range(size)])]
    ppermute x0 -> x30, waiting for transfers between devices: none -> 94.1 us  [exchange(): return lax.ppermute(value, axis, [(i, i ^ bit) for i in range(size)])]
    all_to_all x2, starting transfers between devices: 7.86 us -> 17.8 us  [reorder(): spread = lax.all_to_all(chunks, GROUP, 0, 0, tiled=True)]
    all_to_all x2, waiting for transfers between devices: 7.18 us -> 0.01 us  [reorder(): lax.all_to_all(picked, GROUP, 0, 0, tiled=True).reshape(GEN, feat_here)]
  transfers between devices with their start and end apart: 11 -> 34, of which waited for: 9 -> 24; matrix products, arithmetic and copies ran while one was open for 7% -> 11% of each run, Pallas kernels for 0% -> 0%
where the time goes in v2:
time: 391 us; the launch traced here: 389 us
  starting transfers between devices  143 us (37%)
  waiting for transfers between devices  94.6 us (24%)
  blocking collectives  67.7 us (17%)
  local copies, waits for them, and re-layouts  39.4 us (10%)
  other arithmetic  26.2 us (7%)
  matrix products  10.6 us (3%)
  between operations  7.55 us (2%)
    ppermute x30, starting transfers between devices, exchange(): return lax.ppermute(value, axis, [(i, i ^ bit) for i in range(size)])  112 us
    ppermute x30, waiting for transfers between devices, exchange(): return lax.ppermute(value, axis, [(i, i ^ bit) for i in range(size)])  94.1 us
    pmax x3, blocking collectives, nested(): value = reduce(value, axis)  36.2 us
    psum x3, blocking collectives, nested(): value = reduce(value, axis)  31.5 us
    all_to_all x2, starting transfers between devices, reorder(): spread = lax.all_to_all(chunks, GROUP, 0, 0, tiled=True)  17.8 us
    all_to_all x2, starting transfers between devices, reorder(): lax.all_to_all(picked, GROUP, 0, 0, tiled=True).reshape(GEN, feat_here)  13.1 us
  transfers between devices with their start and end apart: 34, of which 24 were waited for; matrix products, arithmetic and copies ran while one was open for 11% of the time, Pallas kernels for 0%

profile of v2, /device:TPU:1, one launch (start us, length us, event | category | flops | bytes accessed | tf_op | source)
XLA Modules:
  0.0 388.8 jit_solution(9279688031685674822)
XLA Ops:
  3.2 9.0 %psum.21 = f32[256,2]{0,1:T(2,128)S(1)} all-reduce(f32[256,2]{0,1:T(2,128)S(1)} %pad_maximum_fusion.2), channel_id=1, replica_groups=mesh['head'=8,'z'=8,'x'=4,'core'=2] {'core'}, use_global_device_ids=true, to_apply=%region_5.6 | all-reduce | flops 512 | bytes 4096 | tf_op jit(solution)/shard_map/psum | solution.py:26
  12.2 6.1 %psum.22 = f32[256,2]{0,1:T(2,128)S(1)} all-reduce(f32[256,2]{0,1:T(2,128)S(1)} %psum.21), channel_id=1, replica_groups=mesh['head'=8,'z'=8,'x'=4,'core'=2] {'x'}, use_global_device_ids=true, to_apply=%region_6.7 | all-reduce | flops 512 | bytes 4096 | tf_op jit(solution)/shard_map/psum | solution.py:26
  18.2 16.4 %psum.23 = f32[256,2]{0,1:T(2,128)S(1)} all-reduce(f32[256,2]{0,1:T(2,128)S(1)} %psum.22), channel_id=1, replica_groups=mesh['head'=8,'z'=8,'x'=4,'core'=2] {'z'}, use_global_device_ids=true, to_apply=%region_7.8 | all-reduce | flops 512 | bytes 4096 | tf_op jit(solution)/shard_map/psum | solution.py:26
  38.5 8.0 %collective-permute-start = (f32[128,2688]{1,0:T(8,128)}, f32[128,2688]{1,0:T(8,128)}, u32[]{:S(2)}, u32[]{:S(2)}) collective-permute-start(f32[128,2688]{1,0:T(8,128)} %slice_select_fusion), channel_id=1, source_target_pairs={{0,1},{1,0},{2,3},{3,2},{4,5},{5,4},{6,7},{7,6},{8,9},{9,8},{10,11... | collective-permute-start | bytes 4128776 | tf_op jit(solution)/shard_map/ppermute | solution.py:43
  59.7 13.7 %collective-permute-done.1 = f32[64,2688]{1,0:T(8,128)S(1)} collective-permute-done((f32[64,2688]{1,0:T(8,128)S(1)}, f32[64,2688]{1,0:T(8,128)S(1)}, u32[]{:S(2)}, u32[]{:S(2)}) %collective-permute-start.1) | collective-permute-done | bytes 688160 | tf_op jit(solution)/shard_map/ppermute | solution.py:43
  76.4 9.3 %collective-permute-done.2 = f32[32,2688]{1,0:T(8,128)S(1)} collective-permute-done((f32[32,2688]{1,0:T(8,128)S(1)}, f32[32,2688]{1,0:T(8,128)S(1)}, u32[]{:S(2)}, u32[]{:S(2)}) %collective-permute-start.2) | collective-permute-done | bytes 344096 | tf_op jit(solution)/shard_map/ppermute | solution.py:43
  94.0 4.8 %collective-permute-done.4 = f32[8,2688]{1,0:T(8,128)S(1)} collective-permute-done((f32[8,2688]{1,0:T(8,128)S(1)}, f32[8,2688]{1,0:T(8,128)S(1)}, u32[]{:S(2)}, u32[]{:S(2)}) %collective-permute-start.4) | collective-permute-done | bytes 86048 | tf_op jit(solution)/shard_map/ppermute | solution.py:43
  102.2 5.3 %collective-permute-done.5 = f32[4,2688]{1,0:T(4,128)S(1)} collective-permute-done((f32[4,2688]{1,0:T(4,128)S(1)}, f32[4,2688]{1,0:T(4,128)S(1)}, u32[]{:S(2)}, u32[]{:S(2)}) %collective-permute-start.5) | collective-permute-done | bytes 43040 | tf_op jit(solution)/shard_map/ppermute | solution.py:43
  111.5 4.5 %collective-permute-done.6 = bf16[4,2688]{1,0:T(4,128)(2,1)S(1)} collective-permute-done((bf16[4,2688]{1,0:T(4,128)(2,1)S(1)}, bf16[4,2688]{1,0:T(4,128)(2,1)S(1)}, u32[]{:S(2)}, u32[]{:S(2)}) %collective-permute-start.6) | collective-permute-done | bytes 21536 | tf_op jit(solution)/shard_map/ppermute | solution.py:43
  129.5 5.2 %collective-permute-done.9 = bf16[32,2688]{1,0:T(8,128)(2,1)S(1)} collective-permute-done((bf16[32,2688]{1,0:T(8,128)(2,1)S(1)}, bf16[32,2688]{1,0:T(8,128)(2,1)S(1)}, u32[]{:S(2)}, u32[]{:S(2)}) %collective-permute-start.9) | collective-permute-done | bytes 172064 | tf_op jit(solution)/shard_map/ppermute | solution.py:43
  144.9 11.6 %collective-permute-start.11 = (bf16[128,2688]{1,0:T(8,128)(2,1)S(1)}, bf16[128,2688]{1,0:T(8,128)(2,1)S(1)}, u32[]{:S(2)}, u32[]{:S(2)}) collective-permute-start(bf16[128,2688]{1,0:T(8,128)(2,1)S(1)} %maximum_select_fusion.1), channel_id=1, source_target_pairs={{0,1},{1,0},{2,3},{3,2},{4,5},{5,4},{6,7},{7,6},{8,9},{9,8},{10,11... | collective-permute-start | bytes 2064392 | tf_op jit(solution)/shard_map/ppermute | solution.py:43
  167.0 5.3 %and_select_fusion.7 = (s32[64]{0:T(128)S(1)}, s32[64]{0:T(128)S(1)}) fusion(s32[]{:T(128)} %bitcast.2, s32[]{:T(128)} %bitcast.3, s32[]{:T(128)} %bitcast.4, s32[]{:T(128)} %bitcast.5, s32[]{:T(128)} %bitcast.6, s32[]{:T(128)} %bitcast.8, s32[]{:T(128)} %bitcast.7, s32[]{:T(128)} %bitcast.1), kind=kLoop, calls=%fused_computation.206 | loop fusion | flops 2560 | bytes 544 | tf_op jit(solution)/shard_map/jit(_take)/select_n | solution.py:145
  185.4 11.4 %pmax.22 = f32[4,64,7]{1,0,2:T(4,128)S(1)} all-reduce(f32[4,64,7]{1,0,2:T(4,128)S(1)} %pmax.21), channel_id=1, replica_groups=mesh['head'=8,'z'=8,'x'=4,'core'=2] {'x'}, use_global_device_ids=true, to_apply=%region_12.14 | all-reduce | flops 1792 | bytes 14336 | tf_op jit(solution)/shard_map/pmax | solution.py:26
  196.8 21.5 %pmax.23 = f32[4,64,7]{1,0,2:T(4,128)S(1)} all-reduce(f32[4,64,7]{1,0,2:T(4,128)S(1)} %pmax.22), channel_id=1, replica_groups=mesh['head'=8,'z'=8,'x'=4,'core'=2] {'z'}, use_global_device_ids=true, to_apply=%region_13.15 | all-reduce | flops 1792 | bytes 14336 | tf_op jit(solution)/shard_map/pmax | solution.py:26
  232.8 12.2 %collective-permute-start.12 = (f32[128,1024]{1,0:T(8,128)S(1)}, f32[128,1024]{1,0:T(8,128)S(1)}, u32[]{:S(2)}, u32[]{:S(2)}) collective-permute-start(f32[128,1024]{1,0:T(8,128)S(1)} %slice_select_fusion.2), channel_id=1, source_target_pairs={{0,1},{1,0},{2,3},{3,2},{4,5},{5,4},{6,7},{7,6},{8,9},{9,8},{10,11... | collective-permute-start | bytes 1572872 | tf_op jit(solution)/shard_map/ppermute | solution.py:43
  249.3 6.9 %collective-permute-done.13 = f32[64,1024]{1,0:T(8,128)S(1)} collective-permute-done((f32[64,1024]{1,0:T(8,128)S(1)}, f32[64,1024]{1,0:T(8,128)S(1)}, u32[]{:S(2)}, u32[]{:S(2)}) %collective-permute-start.13) | collective-permute-done | bytes 262176 | tf_op jit(solution)/shard_map/ppermute | solution.py:43
  274.1 5.6 %collective-permute-start.17 = (f32[4,1024]{1,0:T(4,128)S(1)}, f32[4,1024]{1,0:T(4,128)S(1)}, u32[]{:S(2)}, u32[]{:S(2)}) collective-permute-start(f32[4,1024]{1,0:T(4,128)S(1)} %slice_select_fusion.14), channel_id=1, source_target_pairs={{0,32},{8,40},{16,48},{24,56},{32,0},{40,8},{48,16},{56,24},{1,33}... | collective-permute-start | bytes 49160 | tf_op jit(solution)/shard_map/ppermute | solution.py:43
  279.7 8.2 %all-to-all-start.2 = ((bf16[8,32,896]{2,1,0:T(8,128)(2,1)}), bf16[8,32,896]{2,1,0:T(8,128)(2,1)S(1)}, u32[]{:S(2)}, u32[]{:S(2)}) async-start(bf16[8,32,896]{2,1,0:T(8,128)(2,1)} %bitcast.67), calls=%async_computation.2 | async-start | bytes 917504 | tf_op jit(solution)/shard_map/all_to_all | solution.py:275
  306.4 4.8 %collective-permute-start.21 = (bf16[32,896]{1,0:T(8,128)(2,1)S(1)}, bf16[32,896]{1,0:T(8,128)(2,1)S(1)}, u32[]{:S(2)}, u32[]{:S(2)}) collective-permute-start(bf16[32,896]{1,0:T(8,128)(2,1)S(1)} %maximum_select_fusion.10), channel_id=1, source_target_pairs={{0,4},{2,6},{4,0},{6,2},{1,5},{3,7},{5,1},{7,3},{8,12},{10,14},{12... | collective-permute-start | bytes 172040 | tf_op jit(solution)/shard_map/ppermute | solution.py:43
  316.3 9.6 %all-to-all-start = ((bf16[8,32,896]{2,1,0:T(8,128)(2,1)}), bf16[8,32,896]{2,1,0:T(8,128)(2,1)S(1)}, u32[]{:S(2)}, u32[]{:S(2)}) async-start(bf16[8,32,896]{2,1,0:T(8,128)(2,1)} %bitcast.60), calls=%async_computation | async-start | bytes 917504 | tf_op jit(solution)/shard_map/all_to_all | solution.py:275
  340.0 4.8 %all-to-all-start.3 = ((bf16[8,32,896]{2,1,0:T(8,128)(2,1)}), bf16[8,32,896]{2,1,0:T(8,128)(2,1)S(1)}, u32[]{:S(2)}, u32[]{:S(2)}) async-start(bf16[8,32,896]{2,1,0:T(8,128)(2,1)} %get-tuple-element.42), calls=%async_computation.3 | async-start | bytes 917504 | tf_op jit(solution)/shard_map/all_to_all | solution.py:277
  352.8 5.1 %collective-permute-start.26 = (f32[32,112]{0,1:T(8,128)S(1)}, f32[32,112]{0,1:T(8,128)S(1)}, u32[]{:S(2)}, u32[]{:S(2)}) collective-permute-start(f32[32,112]{0,1:T(8,128)S(1)} %slice_select_fusion.9), channel_id=1, source_target_pairs={{0,256},{64,320},{128,384},{192,448},{256,0},{320,64},{384,128},{4... | collective-permute-start | bytes 43016 | tf_op jit(solution)/shard_map/ppermute | solution.py:43
  361.8 5.2 %collective-permute-start.27 = (f32[32,112]{0,1:T(8,128)S(1)}, f32[32,112]{0,1:T(8,128)S(1)}, u32[]{:S(2)}, u32[]{:S(2)}) collective-permute-start(f32[32,112]{0,1:T(8,128)S(1)} %select_add_fusion.9), channel_id=1, source_target_pairs={{0,256},{64,320},{128,384},{192,448},{256,0},{320,64},{384,128},{4... | collective-permute-start | bytes 43016 | tf_op jit(solution)/shard_map/ppermute | solution.py:43
  367.0 8.3 %all-to-all-start.1 = ((bf16[8,32,896]{2,1,0:T(8,128)(2,1)}), bf16[8,32,896]{2,1,0:T(8,128)(2,1)S(1)}, u32[]{:S(2)}, u32[]{:S(2)}) async-start(bf16[8,32,896]{2,1,0:T(8,128)(2,1)} %get-tuple-element.43), calls=%async_computation.1 | async-start | bytes 917504 | tf_op jit(solution)/shard_map/all_to_all | solution.py:277
  (263 shorter events, 178.5 us)
Async XLA Ops:
  38.5 12.9 %collective-permute-start = (f32[128,2688]{1,0:T(8,128)}, f32[128,2688]{1,0:T(8,128)}, u32[]{:S(2)}, u32[]{:S(2)}) collective-permute-start(f32[128,2688]{1,0:T(8,128)} %slice_select_fusion), channel_id=1, source_target_pairs={{0,1},{1,0},{2,3},{3,2},{4,5},{5,4},{6,7},{7,6},{8,9},{9,8},{10,11... | collective-permute-start | bytes 4128776 | tf_op jit(solution)/shard_map/ppermute | solution.py:43
  54.3 19.1 %collective-permute-start.1 = (f32[64,2688]{1,0:T(8,128)S(1)}, f32[64,2688]{1,0:T(8,128)S(1)}, u32[]{:S(2)}, u32[]{:S(2)}) collective-permute-start(f32[64,2688]{1,0:T(8,128)S(1)} %slice_select_fusion.1), channel_id=1, source_target_pairs={{0,2},{2,0},{4,6},{6,4},{1,3},{3,1},{5,7},{7,5},{8,10},{10,8},{12,... | collective-permute-start | bytes 2064392 | tf_op jit(solution)/shard_map/ppermute | solution.py:43
  73.5 12.2 %collective-permute-start.2 = (f32[32,2688]{1,0:T(8,128)S(1)}, f32[32,2688]{1,0:T(8,128)S(1)}, u32[]{:S(2)}, u32[]{:S(2)}) collective-permute-start(f32[32,2688]{1,0:T(8,128)S(1)} %slice_select_fusion.3), channel_id=1, source_target_pairs={{0,4},{2,6},{4,0},{6,2},{1,5},{3,7},{5,1},{7,3},{8,12},{10,14},{12... | collective-permute-start | bytes 1032200 | tf_op jit(solution)/shard_map/ppermute | solution.py:43
  98.9 8.7 %collective-permute-start.5 = (f32[4,2688]{1,0:T(4,128)S(1)}, f32[4,2688]{1,0:T(4,128)S(1)}, u32[]{:S(2)}, u32[]{:S(2)}) collective-permute-start(f32[4,2688]{1,0:T(4,128)S(1)} %slice_select_fusion.12), channel_id=1, source_target_pairs={{0,32},{8,40},{16,48},{24,56},{32,0},{40,8},{48,16},{56,24},{1,33}... | collective-permute-start | bytes 129032 | tf_op jit(solution)/shard_map/ppermute | solution.py:43
  107.6 8.4 %collective-permute-start.6 = (bf16[4,2688]{1,0:T(4,128)(2,1)S(1)}, bf16[4,2688]{1,0:T(4,128)(2,1)S(1)}, u32[]{:S(2)}, u32[]{:S(2)}) collective-permute-start(bf16[4,2688]{1,0:T(4,128)(2,1)S(1)} %add_convert_fusion.1), channel_id=1, source_target_pairs={{0,32},{8,40},{16,48},{24,56},{32,0},{40,8},{48,16},{56,24},{1,33}... | collective-permute-start | bytes 64520 | tf_op jit(solution)/shard_map/ppermute | solution.py:43
  127.0 7.7 %collective-permute-start.9 = (bf16[32,2688]{1,0:T(8,128)(2,1)S(1)}, bf16[32,2688]{1,0:T(8,128)(2,1)S(1)}, u32[]{:S(2)}, u32[]{:S(2)}) collective-permute-start(bf16[32,2688]{1,0:T(8,128)(2,1)S(1)} %maximum_select_fusion.6), channel_id=1, source_target_pairs={{0,4},{2,6},{4,0},{6,2},{1,5},{3,7},{5,1},{7,3},{8,12},{10,14},{12... | collective-permute-start | bytes 516104 | tf_op jit(solution)/shard_map/ppermute | solution.py:43
  134.7 10.0 %collective-permute-start.10 = (bf16[64,2688]{1,0:T(8,128)(2,1)S(1)}, bf16[64,2688]{1,0:T(8,128)(2,1)S(1)}, u32[]{:S(2)}, u32[]{:S(2)}) collective-permute-start(bf16[64,2688]{1,0:T(8,128)(2,1)S(1)} %maximum_select_fusion.4), channel_id=1, source_target_pairs={{0,2},{2,0},{4,6},{6,4},{1,3},{3,1},{5,7},{7,5},{8,10},{10,8},{12,... | collective-permute-start | bytes 1032200 | tf_op jit(solution)/shard_map/ppermute | solution.py:43
  144.9 27.6 %collective-permute-start.11 = (bf16[128,2688]{1,0:T(8,128)(2,1)S(1)}, bf16[128,2688]{1,0:T(8,128)(2,1)S(1)}, u32[]{:S(2)}, u32[]{:S(2)}) collective-permute-start(bf16[128,2688]{1,0:T(8,128)(2,1)S(1)} %maximum_select_fusion.1), channel_id=1, source_target_pairs={{0,1},{1,0},{2,3},{3,2},{4,5},{5,4},{6,7},{7,6},{8,9},{9,8},{10,11... | collective-permute-start | bytes 2064392 | tf_op jit(solution)/shard_map/ppermute | solution.py:43
  232.8 13.7 %collective-permute-start.12 = (f32[128,1024]{1,0:T(8,128)S(1)}, f32[128,1024]{1,0:T(8,128)S(1)}, u32[]{:S(2)}, u32[]{:S(2)}) collective-permute-start(f32[128,1024]{1,0:T(8,128)S(1)} %slice_select_fusion.2), channel_id=1, source_target_pairs={{0,1},{1,0},{2,3},{3,2},{4,5},{5,4},{6,7},{7,6},{8,9},{9,8},{10,11... | collective-permute-start | bytes 1572872 | tf_op jit(solution)/shard_map/ppermute | solution.py:43
  246.7 9.4 %collective-permute-start.13 = (f32[64,1024]{1,0:T(8,128)S(1)}, f32[64,1024]{1,0:T(8,128)S(1)}, u32[]{:S(2)}, u32[]{:S(2)}) collective-permute-start(f32[64,1024]{1,0:T(8,128)S(1)} %slice_select_fusion.4), channel_id=1, source_target_pairs={{0,2},{2,0},{4,6},{6,4},{1,3},{3,1},{5,7},{7,5},{8,10},{10,8},{12,... | collective-permute-start | bytes 786440 | tf_op jit(solution)/shard_map/ppermute | solution.py:43
  256.2 7.2 %collective-permute-start.14 = (f32[32,1024]{1,0:T(8,128)S(1)}, f32[32,1024]{1,0:T(8,128)S(1)}, u32[]{:S(2)}, u32[]{:S(2)}) collective-permute-start(f32[32,1024]{1,0:T(8,128)S(1)} %slice_select_fusion.6), channel_id=1, source_target_pairs={{0,4},{2,6},{4,0},{6,2},{1,5},{3,7},{5,1},{7,3},{8,12},{10,14},{12... | collective-permute-start | bytes 393224 | tf_op jit(solution)/shard_map/ppermute | solution.py:43
  274.1 13.9 %collective-permute-start.17 = (f32[4,1024]{1,0:T(4,128)S(1)}, f32[4,1024]{1,0:T(4,128)S(1)}, u32[]{:S(2)}, u32[]{:S(2)}) collective-permute-start(f32[4,1024]{1,0:T(4,128)S(1)} %slice_select_fusion.14), channel_id=1, source_target_pairs={{0,32},{8,40},{16,48},{24,56},{32,0},{40,8},{48,16},{56,24},{1,33}... | collective-permute-start | bytes 49160 | tf_op jit(solution)/shard_map/ppermute | solution.py:43
  279.7 36.5 %all-to-all-start.2 = ((bf16[8,32,896]{2,1,0:T(8,128)(2,1)}), bf16[8,32,896]{2,1,0:T(8,128)(2,1)S(1)}, u32[]{:S(2)}, u32[]{:S(2)}) async-start(bf16[8,32,896]{2,1,0:T(8,128)(2,1)} %bitcast.67), calls=%async_computation.2 | async-start | bytes 917504 | tf_op jit(solution)/shard_map/all_to_all | solution.py:275
  288.1 8.3 %collective-permute-start.18 = (bf16[4,896]{1,0:T(4,128)(2,1)S(1)}, bf16[4,896]{1,0:T(4,128)(2,1)S(1)}, u32[]{:S(2)}, u32[]{:S(2)}) collective-permute-start(bf16[4,896]{1,0:T(4,128)(2,1)S(1)} %fusion.33), channel_id=1, source_target_pairs={{0,32},{8,40},{16,48},{24,56},{32,0},{40,8},{48,16},{56,24},{1,33}... | collective-permute-start | bytes 21512 | tf_op jit(solution)/shard_map/ppermute | solution.py:43
  312.9 13.0 %collective-permute-start.22 = (bf16[64,896]{1,0:T(8,128)(2,1)S(1)}, bf16[64,896]{1,0:T(8,128)(2,1)S(1)}, u32[]{:S(2)}, u32[]{:S(2)}) collective-permute-start(bf16[64,896]{1,0:T(8,128)(2,1)S(1)} %maximum_select_fusion.7), channel_id=1, source_target_pairs={{0,2},{2,0},{4,6},{6,4},{1,3},{3,1},{5,7},{7,5},{8,10},{10,8},{12,... | collective-permute-start | bytes 344072 | tf_op jit(solution)/shard_map/ppermute | solution.py:43
  316.3 18.4 %all-to-all-start = ((bf16[8,32,896]{2,1,0:T(8,128)(2,1)}), bf16[8,32,896]{2,1,0:T(8,128)(2,1)S(1)}, u32[]{:S(2)}, u32[]{:S(2)}) async-start(bf16[8,32,896]{2,1,0:T(8,128)(2,1)} %bitcast.60), calls=%async_computation | async-start | bytes 917504 | tf_op jit(solution)/shard_map/all_to_all | solution.py:275
  325.9 9.4 %collective-permute-start.23 = (bf16[128,896]{1,0:T(8,128)(2,1)S(1)}, bf16[128,896]{1,0:T(8,128)(2,1)S(1)}, u32[]{:S(2)}, u32[]{:S(2)}) collective-permute-start(bf16[128,896]{1,0:T(8,128)(2,1)S(1)} %maximum_select_fusion.5), channel_id=1, source_target_pairs={{0,1},{1,0},{2,3},{3,2},{4,5},{5,4},{6,7},{7,6},{8,9},{9,8},{10,11... | collective-permute-start | bytes 688136 | tf_op jit(solution)/shard_map/ppermute | solution.py:43
  335.6 9.1 %collective-permute-start.24 = (f32[128,112]{0,1:T(8,128)S(1)}, f32[128,112]{0,1:T(8,128)S(1)}, u32[]{:S(2)}, u32[]{:S(2)}) collective-permute-start(f32[128,112]{0,1:T(8,128)S(1)} %slice_select_fusion.11), channel_id=1, source_target_pairs={{0,64},{64,0},{128,192},{192,128},{256,320},{320,256},{384,448},{4... | collective-permute-start | bytes 172040 | tf_op jit(solution)/shard_map/ppermute | solution.py:43
  340.0 27.0 %all-to-all-start.3 = ((bf16[8,32,896]{2,1,0:T(8,128)(2,1)}), bf16[8,32,896]{2,1,0:T(8,128)(2,1)S(1)}, u32[]{:S(2)}, u32[]{:S(2)}) async-start(bf16[8,32,896]{2,1,0:T(8,128)(2,1)} %get-tuple-element.42), calls=%async_computation.3 | async-start | bytes 917504 | tf_op jit(solution)/shard_map/all_to_all | solution.py:277
  344.9 7.8 %collective-permute-start.25 = (f32[64,112]{0,1:T(8,128)S(1)}, f32[64,112]{0,1:T(8,128)S(1)}, u32[]{:S(2)}, u32[]{:S(2)}) collective-permute-start(f32[64,112]{0,1:T(8,128)S(1)} %slice_select_fusion.10), channel_id=1, source_target_pairs={{0,128},{64,192},{128,0},{192,64},{256,384},{320,448},{384,256},{4... | collective-permute-start | bytes 86024 | tf_op jit(solution)/shard_map/ppermute | solution.py:43
  352.8 8.9 %collective-permute-start.26 = (f32[32,112]{0,1:T(8,128)S(1)}, f32[32,112]{0,1:T(8,128)S(1)}, u32[]{:S(2)}, u32[]{:S(2)}) collective-permute-start(f32[32,112]{0,1:T(8,128)S(1)} %slice_select_fusion.9), channel_id=1, source_target_pairs={{0,256},{64,320},{128,384},{192,448},{256,0},{320,64},{384,128},{4... | collective-permute-start | bytes 43016 | tf_op jit(solution)/shard_map/ppermute | solution.py:43
  361.8 13.5 %collective-permute-start.27 = (f32[32,112]{0,1:T(8,128)S(1)}, f32[32,112]{0,1:T(8,128)S(1)}, u32[]{:S(2)}, u32[]{:S(2)}) collective-permute-start(f32[32,112]{0,1:T(8,128)S(1)} %select_add_fusion.9), channel_id=1, source_target_pairs={{0,256},{64,320},{128,384},{192,448},{256,0},{320,64},{384,128},{4... | collective-permute-start | bytes 43016 | tf_op jit(solution)/shard_map/ppermute | solution.py:43
  367.0 18.1 %all-to-all-start.1 = ((bf16[8,32,896]{2,1,0:T(8,128)(2,1)}), bf16[8,32,896]{2,1,0:T(8,128)(2,1)S(1)}, u32[]{:S(2)}, u32[]{:S(2)}) async-start(bf16[8,32,896]{2,1,0:T(8,128)(2,1)} %get-tuple-element.43), calls=%async_computation.1 | async-start | bytes 917504 | tf_op jit(solution)/shard_map/all_to_all | solution.py:277
  375.4 7.7 %collective-permute-start.28 = (f32[64,112]{0,1:T(8,128)S(1)}, f32[64,112]{0,1:T(8,128)S(1)}, u32[]{:S(2)}, u32[]{:S(2)}) collective-permute-start(f32[64,112]{0,1:T(8,128)S(1)} %maximum_select_fusion.11), channel_id=1, source_target_pairs={{0,128},{64,192},{128,0},{192,64},{256,384},{320,448},{384,256},{4... | collective-permute-start | bytes 86024 | tf_op jit(solution)/shard_map/ppermute | solution.py:43
  (23 other events, 636.6 us)

commit v3 on v1

--- a/solution.py
+++ b/solution.py
@@ -25,6 +25,31 @@
     for axis in reversed(BLK_PARTS):
         value = reduce(value, axis)
     return value
+
+
+def axes_size(axes):
+    size = 1
+    for axis in axes:
+        size *= lax.axis_size(axis)
+    return size
+
+
+def scatter_sum(value, axes):
+    n = axes_size(axes)
+    got = lax.all_to_all(value, axes, 0, 0, tiled=True)
+    return jnp.sum(got.reshape((n, value.shape[0] // n) + value.shape[1:]), axis=0)
+
+
+def gather_rows(value, axes):
+    n = axes_size(axes)
+    copies = jnp.broadcast_to(value[None], (n,) + value.shape).reshape((n * value.shape[0],) + value.shape[1:])
+    return lax.all_to_all(copies, axes, 0, 0, tiled=True)
+
+
+def all_combine(value, axes, combine):
+    n = axes_size(axes)
+    got = gather_rows(value[None], axes)
+    return combine(got.reshape((n,) + value.shape), axis=0)
 
 
 def blk_index():
@@ -84,7 +109,7 @@
 
     rows_in = inputs.astype(jnp.float32).reshape(rows, -1)
     stats = jnp.stack([jnp.sum(rows_in, axis=1), jnp.sum(rows_in * rows_in, axis=1)], axis=1)
-    stats = nested(lax.psum, stats)
+    stats = all_combine(stats, BLK_PARTS, jnp.sum)
     row_mean = stats[:, 0] / D
     variance = stats[:, 1] / D - row_mean * row_mean
     normed = (
@@ -95,7 +120,9 @@
     weights_all = jnp.concatenate([w_query, w_key, w_value], axis=1)
     bias_all = jnp.concatenate([b_query, b_key, b_value]).astype(jnp.float32)
     partial = jnp.dot(normed, weights_all, preferred_element_type=jnp.float32)
-    projected = (nested(lax.psum, partial) + bias_all[None, :]).astype(jnp.bfloat16)
+    blk_stages = BLK_PARTS
+    projected = (scatter_sum(partial, blk_stages) + bias_all[None, :]).astype(jnp.bfloat16)
+    projected = gather_rows(projected, blk_stages)
     queries = projected[:, :feat_here].reshape(steps, batch, heads_here, HEAD_DIM)
     key_new = projected[:, feat_here : 2 * feat_here].reshape(steps, batch, feat_here)
     value_new = projected[:, 2 * feat_here :].reshape(steps, batch, feat_here)
@@ -164,7 +191,7 @@
     local_top = lax.dynamic_update_slice_in_dim(local_top, group_top, first_beam, axis=1)
     own_top = jnp.maximum(lax.dynamic_index_in_dim(local_top, own_beam, axis=1, keepdims=True), new_top[:, None])
     local_top = lax.dynamic_update_slice_in_dim(local_top, own_top, own_beam, axis=1)
-    top = nested(lax.pmax, local_top)
+    top = all_combine(local_top, BLK_PARTS, jnp.max)
 
     prompt_weights = jnp.where(
         prompt_live, jnp.exp(prompt_scores - top[:, :, :, None]), 0.0
@@ -212,12 +239,15 @@
         ],
         axis=1,
     )
-    packed = nested(lax.psum, packed)
-    weighted = packed[:, :feat_here].reshape(rows, heads_here, HEAD_DIM)
+    packed = scatter_sum(packed, blk_stages)
+    part_rows = packed.shape[0]
+    weighted = packed[:, :feat_here].reshape(part_rows, heads_here, HEAD_DIM)
     totals = packed[:, feat_here : feat_here + heads_here]
-    attention = (weighted / totals[:, :, None]).reshape(rows, feat_here).astype(jnp.bfloat16)
+    attention = (weighted / totals[:, :, None]).reshape(part_rows, feat_here).astype(jnp.bfloat16)
+    attention = gather_rows(attention, blk_stages)
     head_terms = jnp.dot(attention, w_out, preferred_element_type=jnp.float32)
-    head_total = lax.psum(head_terms, "head")
+    head_stages = ("head",)
+    head_total = gather_rows(scatter_sum(head_terms, head_stages), head_stages)
     hidden = (head_total + b_out.astype(jnp.float32)[None, :]).astype(jnp.bfloat16)
     hidden = hidden.reshape(steps, batch, -1)
 

time: 612 us -> 347 us (0.57)
  waiting for transfers between devices: 415 us -> 141 us
  starting transfers between devices: 18.2 us -> 69.1 us
  blocking collectives: 73.4 us -> 34.5 us
  local copies, waits for them, and re-layouts: 41.3 us -> 55.2 us
  between operations: 20.1 us -> 6.81 us
    psum x7 -> x0, waiting for transfers between devices: 406 us -> none  [the longest x6 333 us: nested(): value = reduce(value, axis)]
    all_to_all x0 -> x7, waiting for transfers between devices: none -> 117 us  [the longest x2 67.6 us: scatter_sum(): got = lax.all_to_all(value, axes, 0, 0, tiled=True)]
    all_to_all x0 -> x7, starting transfers between devices: none -> 48.9 us  [the longest x5 37.4 us: gather_rows(): return lax.all_to_all(copies, axes, 0, 0, tiled=True)]
    pmax x3 -> x0, blocking collectives: 41.9 us -> none  [nested(): value = reduce(value, axis)]
    all_to_all x0 -> x1, blocking collectives: none -> 34.5 us  [scatter_sum(): got = lax.all_to_all(value, axes, 0, 0, tiled=True)]
    psum x3 -> x0, blocking collectives: 31.5 us -> none  [nested(): value = reduce(value, axis)]
    all_to_all x2, waiting for transfers between devices: 1.9 us -> 17.2 us  [reorder(): spread = lax.all_to_all(chunks, GROUP, 0, 0, tiled=True)]
    unnamed x25 -> x35, local copies, waits for them, and re-layouts: 4.22 us -> 11 us
  transfers between devices with their start and end apart: 11 -> 11, of which waited for: 9 -> 11; matrix products, arithmetic and copies ran while one was open for 7% -> 14% of each run, Pallas kernels for 0% -> 0%
where the time goes in v3:
time: 347 us; the launch traced here: 345 us
  waiting for transfers between devices  141 us (41%)
  starting transfers between devices  69.1 us (20%)
  local copies, waits for them, and re-layouts  55.2 us (16%)
  blocking collectives  34.5 us (10%)
  other arithmetic  27.8 us (8%)
  matrix products  11.2 us (3%)
  between operations  6.81 us (2%)
    all_to_all x2, waiting for transfers between devices, scatter_sum(): got = lax.all_to_all(value, axes, 0, 0, tiled=True)  67.6 us
    all_to_all x5, waiting for transfers between devices, gather_rows(): return lax.all_to_all(copies, axes, 0, 0, tiled=True)  49.1 us
    all_to_all x5, starting transfers between devices, gather_rows(): return lax.all_to_all(copies, axes, 0, 0, tiled=True)  37.4 us
    all_to_all x1, blocking collectives, scatter_sum(): got = lax.all_to_all(value, axes, 0, 0, tiled=True)  34.5 us
    all_to_all x2, waiting for transfers between devices, reorder(): spread = lax.all_to_all(chunks, GROUP, 0, 0, tiled=True)  17.2 us
    all_to_all x2, starting transfers between devices, scatter_sum(): got = lax.all_to_all(value, axes, 0, 0, tiled=True)  11.5 us
    unnamed x35, local copies, waits for them, and re-layouts  11 us
    all_to_all x2, starting transfers between devices, reorder(): lax.all_to_all(picked, GROUP, 0, 0, tiled=True).reshape(GEN, feat_here)  10.3 us
  transfers between devices with their start and end apart: 11, of which 11 were waited for; matrix products, arithmetic and copies ran while one was open for 14% of the time, Pallas kernels for 0%

profile of v3, /device:TPU:1, one launch (start us, length us, event | category | flops | bytes accessed | tf_op | source)
XLA Modules:
  0.0 345.3 jit_solution(4549313372943214596)
XLA Ops:
  2.5 14.8 %all-to-all-start = ((f32[64,256,2]{1,2,0:T(2,128)}), f32[64,256,2]{1,2,0:T(2,128)S(1)}, u32[]{:S(2)}, u32[]{:S(2)}) async-start(f32[64,256,2]{1,2,0:T(2,128)} %reshape.585), calls=%async_computation | async-start | bytes 262144 | tf_op jit(solution)/shard_map/all_to_all | solution.py:46
  19.6 8.9 %all-to-all-done = f32[64,256,2]{1,2,0:T(2,128)S(1)} async-done(((f32[64,256,2]{1,2,0:T(2,128)}), f32[64,256,2]{1,2,0:T(2,128)S(1)}, u32[]{:S(2)}, u32[]{:S(2)}) %all-to-all-start) | async-done | bytes 131104 | tf_op jit(solution)/shard_map/all_to_all | solution.py:46
  34.1 4.7 %all-to-all-start.1 = ((f32[64,4,2688]{2,1,0:T(4,128)}), f32[64,4,2688]{2,1,0:T(4,128)S(1)}, u32[]{:S(2)}, u32[]{:S(2)}) async-start(f32[64,4,2688]{2,1,0:T(4,128)} %copy.116), calls=%async_computation.1 | async-start | bytes 5505024 | tf_op jit(solution)/shard_map/all_to_all | solution.py:39
  43.3 59.8 %all-to-all-done.1 = f32[64,4,2688]{2,1,0:T(4,128)S(1)} async-done(((f32[64,4,2688]{2,1,0:T(4,128)}), f32[64,4,2688]{2,1,0:T(4,128)S(1)}, u32[]{:S(2)}, u32[]{:S(2)}) %all-to-all-start.1) | async-done | bytes 2752544 | tf_op jit(solution)/shard_map/all_to_all | solution.py:39
  105.1 6.5 %all-to-all-start.2 = ((bf16[64,4,2688]{2,1,0:T(4,128)(2,1)}), bf16[64,4,2688]{2,1,0:T(4,128)(2,1)S(1)}, u32[]{:S(2)}, u32[]{:S(2)}) async-start(bf16[64,4,2688]{2,1,0:T(4,128)(2,1)} %broadcast_in_dim.197), calls=%async_computation.2 | async-start | bytes 2752512 | tf_op jit(solution)/shard_map/all_to_all | solution.py:46
  130.2 5.1 %and_select_fusion.7 = (s32[64]{0:T(128)S(1)}, s32[64]{0:T(128)S(1)}) fusion(s32[]{:T(128)} %bitcast.2, s32[]{:T(128)} %bitcast.3, s32[]{:T(128)} %bitcast.4, s32[]{:T(128)} %bitcast.5, s32[]{:T(128)} %bitcast.6, s32[]{:T(128)} %bitcast.8, s32[]{:T(128)} %bitcast.7, s32[]{:T(128)} %bitcast.1), kind=kLoop, calls=%fused_computation.161 | loop fusion | flops 2560 | bytes 544 | tf_op jit(solution)/shard_map/jit(_take)/select_n | solution.py:131
  135.6 11.0 %all-to-all-done.2 = bf16[64,4,2688]{2,1,0:T(4,128)(2,1)S(1)} async-done(((bf16[64,4,2688]{2,1,0:T(4,128)(2,1)}), bf16[64,4,2688]{2,1,0:T(4,128)(2,1)S(1)}, u32[]{:S(2)}, u32[]{:S(2)}) %all-to-all-start.2) | async-done | bytes 1376288 | tf_op jit(solution)/shard_map/all_to_all | solution.py:46
  159.7 7.4 %all-to-all-start.3 = ((f32[64,1,1792]{2,1,0:T(1,128)}), f32[64,1,1792]{2,1,0:T(1,128)}, u32[]{:S(2)}, u32[]{:S(2)}) async-start(f32[64,1,1792]{2,1,0:T(1,128)} %reshape.837), calls=%async_computation.3 | async-start | bytes 917504 | tf_op jit(solution)/shard_map/all_to_all | solution.py:46
  173.5 10.0 %all-to-all-done.3 = f32[64,1,1792]{2,1,0:T(1,128)} async-done(((f32[64,1,1792]{2,1,0:T(1,128)}), f32[64,1,1792]{2,1,0:T(1,128)}, u32[]{:S(2)}, u32[]{:S(2)}) %all-to-all-start.3) | async-done | bytes 458784 | tf_op jit(solution)/shard_map/all_to_all | solution.py:46
  184.0 3.5 %reduce.40 = f32[64,1792]{1,0:T(8,128)} reduce(f32[64,1,1792]{2,1,0:T(1,128)} %all-to-all-done.3, f32[]{:T(128)} %broadcast.563), dimensions={1}, to_apply=%all_to_all.50.reduce_sub_computation | reduce | bytes 917508 | tf_op jit(solution)/shard_map/all_to_all | solution.py:46
  205.9 34.5 %all_to_all.72 = f32[64,4,1024]{2,1,0:T(4,128)S(1)} all-to-all(f32[64,4,1024]{2,1,0:T(4,128)S(1)} %pad_maximum_fusion), channel_id=1, replica_groups=mesh['head'=8,'z'=8,'x'=4,'core'=2] {'z','x','core'}, dimensions={0} | all-to-all | bytes 2097152 | tf_op jit(solution)/shard_map/all_to_all | solution.py:39
  240.4 5.6 %all-to-all-start.10 = ((bf16[8,32,896]{2,1,0:T(8,128)(2,1)}), bf16[8,32,896]{2,1,0:T(8,128)(2,1)S(1)}, u32[]{:S(2)}, u32[]{:S(2)}) async-start(bf16[8,32,896]{2,1,0:T(8,128)(2,1)} %bitcast.67), calls=%async_computation.10 | async-start | bytes 917504 | tf_op jit(solution)/shard_map/all_to_all | solution.py:261
  246.3 8.5 %all-to-all-done.10 = bf16[8,32,896]{2,1,0:T(8,128)(2,1)S(1)} async-done(((bf16[8,32,896]{2,1,0:T(8,128)(2,1)}), bf16[8,32,896]{2,1,0:T(8,128)(2,1)S(1)}, u32[]{:S(2)}, u32[]{:S(2)}) %all-to-all-start.10) | async-done | bytes 458784 | tf_op jit(solution)/shard_map/all_to_all | solution.py:261
  254.8 4.2 %all-to-all-start.8 = ((bf16[8,32,896]{2,1,0:T(8,128)(2,1)}), bf16[8,32,896]{2,1,0:T(8,128)(2,1)S(1)}, u32[]{:S(2)}, u32[]{:S(2)}) async-start(bf16[8,32,896]{2,1,0:T(8,128)(2,1)} %bitcast.60), calls=%async_computation.8 | async-start | bytes 917504 | tf_op jit(solution)/shard_map/all_to_all | solution.py:261
  259.1 8.7 %all-to-all-done.8 = bf16[8,32,896]{2,1,0:T(8,128)(2,1)S(1)} async-done(((bf16[8,32,896]{2,1,0:T(8,128)(2,1)}), bf16[8,32,896]{2,1,0:T(8,128)(2,1)S(1)}, u32[]{:S(2)}, u32[]{:S(2)}) %all-to-all-start.8) | async-done | bytes 458784 | tf_op jit(solution)/shard_map/all_to_all | solution.py:261
  268.7 5.2 %all-to-all-start.5 = ((bf16[64,4,896]{2,1,0:T(4,128)(2,1)}), bf16[64,4,896]{2,1,0:T(4,128)(2,1)S(1)}, u32[]{:S(2)}, u32[]{:S(2)}) async-start(bf16[64,4,896]{2,1,0:T(4,128)(2,1)} %broadcast_in_dim.210), calls=%async_computation.5 | async-start | bytes 917504 | tf_op jit(solution)/shard_map/all_to_all | solution.py:46
  277.6 12.7 %all-to-all-done.5 = bf16[64,4,896]{2,1,0:T(4,128)(2,1)S(1)} async-done(((bf16[64,4,896]{2,1,0:T(4,128)(2,1)}), bf16[64,4,896]{2,1,0:T(4,128)(2,1)S(1)}, u32[]{:S(2)}, u32[]{:S(2)}) %all-to-all-start.5) | async-done | bytes 458784 | tf_op jit(solution)/shard_map/all_to_all | solution.py:46
  290.4 4.6 %all-to-all-start.11 = ((bf16[8,32,896]{2,1,0:T(8,128)(2,1)}), bf16[8,32,896]{2,1,0:T(8,128)(2,1)S(1)}, u32[]{:S(2)}, u32[]{:S(2)}) async-start(bf16[8,32,896]{2,1,0:T(8,128)(2,1)} %get-tuple-element.42), calls=%async_computation.11 | async-start | bytes 917504 | tf_op jit(solution)/shard_map/all_to_all | solution.py:263
  303.7 6.8 %all-to-all-start.6 = ((f32[8,32,112]{2,1,0:T(8,128)}), f32[8,32,112]{2,1,0:T(8,128)S(1)}, u32[]{:S(2)}, u32[]{:S(2)}) async-start(f32[8,32,112]{2,1,0:T(8,128)} %fusion.16), calls=%async_computation.6 | async-start | bytes 262144 | tf_op jit(solution)/shard_map/all_to_all | solution.py:39
  310.5 7.8 %all-to-all-done.6 = f32[8,32,112]{2,1,0:T(8,128)S(1)} async-done(((f32[8,32,112]{2,1,0:T(8,128)}), f32[8,32,112]{2,1,0:T(8,128)S(1)}, u32[]{:S(2)}, u32[]{:S(2)}) %all-to-all-start.6) | async-done | bytes 114720 | tf_op jit(solution)/shard_map/all_to_all | solution.py:39
  318.4 5.8 %all-to-all-start.9 = ((bf16[8,32,896]{2,1,0:T(8,128)(2,1)}), bf16[8,32,896]{2,1,0:T(8,128)(2,1)S(1)}, u32[]{:S(2)}, u32[]{:S(2)}) async-start(bf16[8,32,896]{2,1,0:T(8,128)(2,1)} %get-tuple-element.43), calls=%async_computation.9 | async-start | bytes 917504 | tf_op jit(solution)/shard_map/all_to_all | solution.py:263
  328.2 4.7 %all-to-all-done.9 = bf16[8,32,896]{2,1,0:T(8,128)(2,1)S(1)} async-done(((bf16[8,32,896]{2,1,0:T(8,128)(2,1)}), bf16[8,32,896]{2,1,0:T(8,128)(2,1)S(1)}, u32[]{:S(2)}, u32[]{:S(2)}) %all-to-all-start.9) | async-done | bytes 458784 | tf_op jit(solution)/shard_map/all_to_all | solution.py:263
  333.6 3.4 all-to-all-start.7
  338.2 6.4 %all-to-all-done.7 = f32[8,32,112]{2,1,0:T(8,128)S(1)} async-done(((f32[8,32,112]{2,1,0:T(8,128)}), f32[8,32,112]{2,1,0:T(8,128)S(1)}, u32[]{:S(2)}, u32[]{:S(2)}) %all-to-all-start.7) | async-done | bytes 114720 | tf_op jit(solution)/shard_map/all_to_all | solution.py:46
  (193 shorter events, 87.6 us)
Async XLA Ops:
  0.6 300.1 %copy-start = (bf16[896,112]{0,1:T(8,128)(2,1)S(1)}, bf16[896,112]{0,1:T(8,128)(2,1)}, u32[]{:S(2)}) copy-start(bf16[896,112]{0,1:T(8,128)(2,1)} %param.34) | copy-start | bytes 602116
  2.5 26.0 %all-to-all-start = ((f32[64,256,2]{1,2,0:T(2,128)}), f32[64,256,2]{1,2,0:T(2,128)S(1)}, u32[]{:S(2)}, u32[]{:S(2)}) async-start(f32[64,256,2]{1,2,0:T(2,128)} %reshape.585), calls=%async_computation | async-start | bytes 262144 | tf_op jit(solution)/shard_map/all_to_all | solution.py:46
  34.1 4.8 %copy-start.7 = (s32[4,64]{1,0:T(4,128)S(1)}, s32[4,64]{1,0:T(4,128)}, u32[]{:S(2)}) copy-start(s32[4,64]{1,0:T(4,128)} %param.43) | copy-start | bytes 3076
  34.1 8.8 %copy-start.4 = (bf16[896]{0:T(1024)(128)(2,1)S(1)}, bf16[896]{0:T(1024)(128)(2,1)}, u32[]{:S(2)}) copy-start(bf16[896]{0:T(1024)(128)(2,1)} %param.33) | copy-start | bytes 5380
  34.1 8.8 %copy-start.5 = (bf16[896]{0:T(1024)(128)(2,1)S(1)}, bf16[896]{0:T(1024)(128)(2,1)}, u32[]{:S(2)}) copy-start(bf16[896]{0:T(1024)(128)(2,1)} %param.32) | copy-start | bytes 5380
  34.1 8.8 %copy-start.6 = (bf16[896]{0:T(1024)(128)(2,1)S(1)}, bf16[896]{0:T(1024)(128)(2,1)}, u32[]{:S(2)}) copy-start(bf16[896]{0:T(1024)(128)(2,1)} %param.31) | copy-start | bytes 5380
  34.1 8.8 %copy-start.2 = (s32[8]{0:T(128)S(1)}, s32[8]{0:T(128)}, u32[]{:S(2)}) copy-start(s32[8]{0:T(128)} %param.41) | copy-start | bytes 100
  34.1 8.9 %copy-start.3 = (s32[8,288]{1,0:T(8,128)S(1)}, s32[8,288]{1,0:T(8,128)}, u32[]{:S(2)}) copy-start(s32[8,288]{1,0:T(8,128)} %param.40) | copy-start | bytes 27652
  34.1 69.0 %all-to-all-start.1 = ((f32[64,4,2688]{2,1,0:T(4,128)}), f32[64,4,2688]{2,1,0:T(4,128)S(1)}, u32[]{:S(2)}, u32[]{:S(2)}) async-start(f32[64,4,2688]{2,1,0:T(4,128)} %copy.116), calls=%async_computation.1 | async-start | bytes 5505024 | tf_op jit(solution)/shard_map/all_to_all | solution.py:39
  103.6 9.2 %copy-start.1 = (bf16[24,16,896]{2,1,0:T(8,128)(2,1)S(1)}, bf16[24,16,896]{2,1,0:T(8,128)(2,1)}, u32[]{:S(2)}) copy-start(bf16[24,16,896]{2,1,0:T(8,128)(2,1)} %param.36) | copy-start | bytes 2064388
  105.1 41.5 %all-to-all-start.2 = ((bf16[64,4,2688]{2,1,0:T(4,128)(2,1)}), bf16[64,4,2688]{2,1,0:T(4,128)(2,1)S(1)}, u32[]{:S(2)}, u32[]{:S(2)}) async-start(bf16[64,4,2688]{2,1,0:T(4,128)(2,1)} %broadcast_in_dim.197), calls=%async_computation.2 | async-start | bytes 2752512 | tf_op jit(solution)/shard_map/all_to_all | solution.py:46
  111.6 15.9 %copy-start.12 = (s32[8]{0:T(128)S(1)}, s32[8]{0:T(128)}, u32[]{:S(2)}) copy-start(s32[8]{0:T(128)} %param.42) | copy-start | bytes 100
  149.3 5.7 %copy-start.10 = (pred[4,4]{1,0:T(4,128)(4,1)S(1)}, pred[4,4]{1,0:T(4,128)(4,1)}, u32[]{:S(2)}) copy-start(pred[4,4]{1,0:T(4,128)(4,1)} %iota_compare_fusion.1) | copy-start | bytes 52
  159.7 23.8 %all-to-all-start.3 = ((f32[64,1,1792]{2,1,0:T(1,128)}), f32[64,1,1792]{2,1,0:T(1,128)}, u32[]{:S(2)}, u32[]{:S(2)}) async-start(f32[64,1,1792]{2,1,0:T(1,128)} %reshape.837), calls=%async_computation.3 | async-start | bytes 917504 | tf_op jit(solution)/shard_map/all_to_all | solution.py:46
  187.5 5.7 %copy-start.11 = (pred[4,4]{1,0:T(4,128)(4,1)S(1)}, pred[4,4]{1,0:T(4,128)(4,1)}, u32[]{:S(2)}) copy-start(pred[4,4]{1,0:T(4,128)(4,1)} %iota_compare_fusion.1) | copy-start | bytes 52
  205.6 40.4 %copy-start.9 = (s32[64]{0:T(128)S(1)}, s32[64]{0:T(128)}, u32[]{:S(2)}) copy-start(s32[64]{0:T(128)} %copy-done.8) | copy-start | bytes 772
  240.4 14.4 %all-to-all-start.10 = ((bf16[8,32,896]{2,1,0:T(8,128)(2,1)}), bf16[8,32,896]{2,1,0:T(8,128)(2,1)S(1)}, u32[]{:S(2)}, u32[]{:S(2)}) async-start(bf16[8,32,896]{2,1,0:T(8,128)(2,1)} %bitcast.67), calls=%async_computation.10 | async-start | bytes 917504 | tf_op jit(solution)/shard_map/all_to_all | solution.py:261
  254.8 13.0 %all-to-all-start.8 = ((bf16[8,32,896]{2,1,0:T(8,128)(2,1)}), bf16[8,32,896]{2,1,0:T(8,128)(2,1)S(1)}, u32[]{:S(2)}, u32[]{:S(2)}) async-start(bf16[8,32,896]{2,1,0:T(8,128)(2,1)} %bitcast.60), calls=%async_computation.8 | async-start | bytes 917504 | tf_op jit(solution)/shard_map/all_to_all | solution.py:261
  268.7 29.9 %copy-start.13 = (bf16[112]{0:T(256)(128)(2,1)S(1)}, bf16[112]{0:T(256)(128)(2,1)}, u32[]{:S(2)}) copy-start(bf16[112]{0:T(256)(128)(2,1)} %param.35) | copy-start | bytes 676
  268.7 21.6 %all-to-all-start.5 = ((bf16[64,4,896]{2,1,0:T(4,128)(2,1)}), bf16[64,4,896]{2,1,0:T(4,128)(2,1)S(1)}, u32[]{:S(2)}, u32[]{:S(2)}) async-start(bf16[64,4,896]{2,1,0:T(4,128)(2,1)} %broadcast_in_dim.210), calls=%async_computation.5 | async-start | bytes 917504 | tf_op jit(solution)/shard_map/all_to_all | solution.py:46
  290.4 13.3 %all-to-all-start.11 = ((bf16[8,32,896]{2,1,0:T(8,128)(2,1)}), bf16[8,32,896]{2,1,0:T(8,128)(2,1)S(1)}, u32[]{:S(2)}, u32[]{:S(2)}) async-start(bf16[8,32,896]{2,1,0:T(8,128)(2,1)} %get-tuple-element.42), calls=%async_computation.11 | async-start | bytes 917504 | tf_op jit(solution)/shard_map/all_to_all | solution.py:263
  303.7 14.7 %all-to-all-start.6 = ((f32[8,32,112]{2,1,0:T(8,128)}), f32[8,32,112]{2,1,0:T(8,128)S(1)}, u32[]{:S(2)}, u32[]{:S(2)}) async-start(f32[8,32,112]{2,1,0:T(8,128)} %fusion.16), calls=%async_computation.6 | async-start | bytes 262144 | tf_op jit(solution)/shard_map/all_to_all | solution.py:39
  318.4 14.6 %all-to-all-start.9 = ((bf16[8,32,896]{2,1,0:T(8,128)(2,1)}), bf16[8,32,896]{2,1,0:T(8,128)(2,1)S(1)}, u32[]{:S(2)}, u32[]{:S(2)}) async-start(bf16[8,32,896]{2,1,0:T(8,128)(2,1)} %get-tuple-element.43), calls=%async_computation.9 | async-start | bytes 917504 | tf_op jit(solution)/shard_map/all_to_all | solution.py:263
  333.6 11.1 %all-to-all-start.7 = ((f32[8,32,112]{2,1,0:T(8,128)}), f32[8,32,112]{2,1,0:T(8,128)S(1)}, u32[]{:S(2)}, u32[]{:S(2)}) async-start(f32[8,32,112]{2,1,0:T(8,128)} %broadcast_in_dim.211), calls=%async_computation.7 | async-start | bytes 262144 | tf_op jit(solution)/shard_map/all_to_all | solution.py:46
  (1 other events, 0.8 us)
